TPU v7x, 128 devices: a whole 4x4x4 slice. The times are simulated.
128 devices in a mesh: win: 16 (over y, x), tile: 8 (over z, core).
Axes of the slice: x: 4, y: 4, z: 4, core: 2. Of those that a mesh axis runs over, the one named last changes fastest.
Arguments:
- spectra: bfloat16 [768, 16, 128, 128], P('win', 'tile'), may hold values from -20 to 20
- segment_ids: int32 [768], P('win'), may hold values from 0 to 95, never falling along the last dimension, each value on 1 to 16 neighbouring positions
- pair_blocks: int32 [24, 2], P('tile'), may hold values from 0 to 15, as said below
- pair_count: int32 [8], P('tile'), may hold values from 2 to 3
Outputs:
- correlations: float32 [24, 128, 64, 128], P('tile', 'win')
Inputs may be any that keep to these rules, and one draw needn't show every extreme that they name: `pair_blocks`: slot r of owner t = r // 3 names blocks a and b with |a - b| <= 2, both among the blocks (t - 1) * 2 to (t + 2) * 2 - 1; every slot holds valid blocks, live or not. `segment_ids`: segment numbers never fall along the windows; each segment spans 1 to 16 windows.
All inputs are finite; a program needn't handle non-finite values.
Results may differ from a plain program's by a relative error of at most 0.00065.
Values may be sent and summed in bfloat16 or wider, within the bound.
No kernel may reach another device: no remote copies, remote signals or barrier semaphores. Data moves between devices by JAX's collectives and lax.ppermute only.
A program may use at most 192 MiB of HBM per device.

v0:
```python
import math

import jax
import jax.numpy as jnp
from jax import lax
from jax.sharding import PartitionSpec as P

FB = 64
SUB = 32
NFFT = 4096
F0 = 64
LAGS = 64


def padded(value, sides, width):
    for axis, dim in sides:
        count, length = (lax.axis_size(axis), value.shape[dim])
        up = [(i, (i + 1) % count) for i in range(count - 1)]
        down = [(j, i) for i, j in up]
        last = lax.slice_in_dim(value, length - width, length, axis=dim)
        initial = lax.slice_in_dim(value, 0, width, axis=dim)
        before = lax.ppermute(last, axis, up)
        after = lax.ppermute(initial, axis, down)
        value = jnp.concatenate([before, value, after], axis=dim)
    return value


def whiten(spectra):
    values = spectra.astype(jnp.float32)
    real_part = values[..., :FB]
    imag_part = values[..., FB:]
    power_sum = real_part * real_part + imag_part * imag_part
    band_power = (
        jnp.mean(power_sum.reshape(power_sum.shape[:-1] + (FB // SUB, SUB)), axis=-1) + 1e-06
    )
    scales = jnp.repeat(1.0 / jnp.sqrt(band_power), SUB, axis=-1)
    both_scales = jnp.concatenate([scales, scales], axis=-1)
    return (values * both_scales).astype(jnp.bfloat16)


def lag_table():
    bins = jnp.arange(FB, dtype=jnp.int32) + F0
    shifts = jnp.arange(LAGS, dtype=jnp.int32) - LAGS // 2
    products = jnp.mod(bins[:, None] * shifts[None, :], NFFT)
    phases = products.astype(jnp.float32) * (2.0 * math.pi / NFFT)
    norm_scale = 1.0 / math.sqrt(FB)
    return jnp.concatenate([jnp.cos(phases), -jnp.sin(phases)], axis=0) * norm_scale


def cross_spectrum(first_block, second_block, weight):
    left = (first_block.astype(jnp.float32) * weight[:, None, None]).astype(jnp.bfloat16)
    left_real, left_imag = (left[..., :FB], left[..., FB:])
    right_real, right_imag = (second_block[..., :FB], second_block[..., FB:])
    left_both = jnp.stack([jnp.stack([left_real, left_imag]), jnp.stack([left_imag, -left_real])])
    right_both = jnp.stack([right_real, right_imag])
    cross = jnp.einsum(
        "qpwcf,pwdf->cqfd", left_both, right_both, preferred_element_type=jnp.float32
    )
    return cross.reshape(cross.shape[0], 2 * FB, cross.shape[3])


def on_device(spectra, segment_ids, pair_blocks, pair_count):
    whitened = whiten(spectra)
    window_count = segment_ids.shape[0]
    segment_total = lax.axis_size("win") * window_count // 8
    labels = jnp.arange(segment_total, dtype=jnp.int32)
    own_hot = (segment_ids[:, None] == labels[None, :]).astype(jnp.float32)
    sizes = lax.psum(jnp.sum(own_hot, axis=0), "win")
    weight = 1.0 / jnp.dot(own_hot, sizes, precision=lax.Precision.HIGHEST)
    block_count = whitened.shape[1]
    extended = padded(whitened, (("tile", 1),), block_count)
    first_local = lax.axis_index("tile") * block_count - block_count
    basis = lag_table()
    slot_total = pair_blocks.shape[0]
    live_count = pair_count[0]

    def slot_cross(slot_index):
        first_block = lax.dynamic_index_in_dim(
            extended, pair_blocks[slot_index, 0] - first_local, 1, keepdims=False
        )
        second_block = lax.dynamic_index_in_dim(
            extended, pair_blocks[slot_index, 1] - first_local, 1, keepdims=False
        )
        return cross_spectrum(first_block, second_block, weight)

    slot_numbers = jnp.arange(slot_total, dtype=jnp.int32)
    stacked = jax.vmap(slot_cross)(slot_numbers)
    live_mask = (slot_numbers < live_count).astype(jnp.float32)
    stacked = stacked * live_mask[:, None, None, None]
    share = lax.psum_scatter(stacked, "win", scatter_dimension=1, tiled=True)
    return jnp.einsum("pcgd,gl->pcld", share, basis, precision=lax.Precision.HIGHEST)


def solution(mesh):
    return jax.shard_map(
        on_device,
        mesh=mesh,
        in_specs=(P("win", "tile", None, None), P("win"), P("tile", None), P("tile")),
        out_specs=P("tile", "win", None, None),
        check_vma=False,
    )
```

profile of v0, /device:TPU:1, one launch (start us, length us, event | category | flops | bytes accessed | tf_op | source)
XLA Modules:
  0.0 505.9 jit_solution(13071203536800000273)
XLA Ops:
  6.5 2.7 copy_convert_fusion
  9.3 4.3 fusion.4
  13.6 4.4 copy.32
  18.0 0.6 bitcast_reduce_fusion
  18.7 0.2 broadcast_in_dim.4
  18.9 4.0 copy.33
  22.9 6.4 %fusion.5 = bf16[48,2,128,128]{3,2,0,1:T(8,128)(2,1)S(1)} fusion(f32[48,2,128,64]{3,2,0,1:T(8,128)} %copy.33, bf16[48,2,128,128]{3,2,1,0:T(8,128)(2,1)} %param.4), kind=kLoop, calls=%fused_computation.16 | loop fusion | flops 6291456 | bytes 9437184 | tf_op jit(solution)/shard_map/convert_element_type | solution.py:38
  29.4 4.9 collective-permute-start
  34.3 1.9 collective-permute-start.1
  36.3 0.7 gather_fusion.2
  36.9 0.7 gather_fusion
  38.4 33.7 %psum.7 = f32[96]{0:T(128)S(1)} all-reduce(f32[96]{0:T(128)S(1)} %convert_reduce_fusion), channel_id=1, replica_groups=mesh['win'=16,'tile'=8] {'win'}, use_global_device_ids=true, to_apply=%region_2.0 | all-reduce | flops 96 | bytes 768 | tf_op jit(solution)/shard_map/psum | solution.py:68
  72.0 0.2 fusion.13
  72.3 0.7 collective-permute-done.1
  73.0 7.7 %pad_maximum_fusion = bf16[48,6,128,128]{3,2,0,1:T(8,128)(2,1)} fusion(bf16[48,2,128,128]{3,2,0,1:T(8,128)(2,1)} %collective-permute-done.1, bf16[48,2,128,128]{3,2,0,1:T(8,128)(2,1)S(1)} %fusion.5, bf16[48,2,128,128]{3,2,0,1:T(8,128)(2,1)} %collective-permute-done), kind=kLoop, calls=%fused_computation.6 | loop fusion | flops 9437184 | bytes 18874368 | tf_op jit(solution)/shard_map/concatenate | solution.py:24
  80.7 7.3 %gather_fusion.3 = bf16[3,48,128,128]{3,2,1,0:T(8,128)(2,1)} fusion(bf16[48,6,128,128]{3,2,0,1:T(8,128)(2,1)} %pad_maximum_fusion, s32[3]{0:T(128)S(1)} %get-tuple-element.14), kind=kCustom, calls=%fused_computation.3 | custom fusion | bytes 9437232 | tf_op jit(solution)/shard_map/vmap(jit(dynamic_index_in_dim))/gather | solution.py:78
  88.0 7.0 %copy.37 = bf16[3,48,128,128]{2,1,3,0:T(8,128)(2,1)} copy(bf16[3,48,128,128]{3,2,1,0:T(8,128)(2,1)} %gather_fusion.3) | data formatting | bytes 9437184 | tf_op jit(solution)/shard_map/vmap(jit(dynamic_index_in_dim))/gather | solution.py:78
  95.0 3.3 fusion.3
  98.3 3.3 slice_bitcast_fusion.2
  101.6 7.3 %gather_fusion.1 = bf16[3,48,128,128]{3,2,1,0:T(8,128)(2,1)} fusion(bf16[48,6,128,128]{3,2,0,1:T(8,128)(2,1)} %pad_maximum_fusion, s32[3]{0:T(128)S(1)} %get-tuple-element.13), kind=kCustom, calls=%fused_computation.1 | custom fusion | bytes 9437232 | tf_op jit(solution)/shard_map/vmap(jit(dynamic_index_in_dim))/gather | solution.py:81
  108.9 9.4 %fusion.35 = (bf16[3,48,128,64]{3,2,1,0:T(8,128)(2,1)}, bf16[3,48,128,64]{3,2,1,0:T(8,128)(2,1)}) fusion(bf16[3,48,128,128]{3,2,1,0:T(8,128)(2,1)} %gather_fusion.1), kind=kLoop, calls=%fused_computation.68 | loop fusion | bytes 9437184 | tf_op jit(solution)/shard_map/vmap()/slice | solution.py:53
  118.3 6.3 %copy.46 = bf16[3,48,128,64]{2,1,3,0:T(8,128)(2,1)} copy(bf16[3,48,128,64]{3,2,1,0:T(8,128)(2,1)} %get-tuple-element.5) | data formatting | bytes 4718592
  124.6 6.2 %copy.47 = bf16[3,48,128,64]{2,1,3,0:T(8,128)(2,1)} copy(bf16[3,48,128,64]{3,2,1,0:T(8,128)(2,1)} %get-tuple-element.6) | data formatting | bytes 4718592
  130.7 2.8 maximum_bitcast_fusion.3
  133.5 12.1 %convolution_bitcast_fusion = f32[3,128,2,64,128]{1,4,2,3,0:T(8,128)} fusion(bf16[1,2,3,48,128,64]{4,3,1,0,5,2:T(8,128)(2,1)S(1)} %maximum_bitcast_fusion.3, bf16[1,3,48,128,64]{3,2,0,4,1:T(8,128)(2,1)} %bitcast.66, bf16[1,3,48,128,64]{3,2,0,4,1:T(8,128)(2,1)} %bitcast.65, bf16[1,3,48,128,64]{3,2,4,1,0:T(8,128)(2,1)} %get-tuple-element.10, ...), kind=kOutput, calls=%fused_computation.5 | convolution fusion | flops 1238630400 | bytes 39321600 | tf_op jit(solution)/shard_map/vmap(qpwcf,pwdf->cqfd)/dot_general | solution.py:56
  145.6 24.8 %copy.40 = f32[3,128,2,64,128]{4,3,2,1,0:T(8,128)} copy(f32[3,128,2,64,128]{1,4,2,3,0:T(8,128)} %convolution_bitcast_fusion) | data formatting | bytes 50331648 | tf_op jit(solution)/shard_map/vmap(qpwcf,pwdf->cqfd)/transpose | solution.py:56
  170.5 17.7 %bitcast_multiply_fusion = f32[3,128,128,128]{3,2,1,0:T(8,128)} fusion(f32[3,128,2,64,128]{4,3,2,1,0:T(8,128)} %copy.40, f32[3]{0:T(128)S(1)} %compare_convert_fusion), kind=kLoop, calls=%fused_computation.4 | loop fusion | flops 6291456 | bytes 50331660 | tf_op jit(solution)/shard_map/mul | solution.py:89
  188.2 0.6 copy-done.4
  188.8 0.6 dynamic-slice
  190.1 0.2 fusion.22
  190.3 305.5 %all-reduce.3.cloned.1.call-done = f32[3,128,128,128]{3,2,1,0:T(8,128)} async-done(((f32[3,128,128,128]{3,2,1,0:T(8,128)}), f32[3,128,128,128]{3,2,1,0:T(8,128)}) %all-reduce.3.cloned.1.call-update) | async-done | bytes 25165840
  495.8 3.2 fusion.10
  (18 shorter events, 0.3 us)
Async XLA Ops:
  6.5 29.7 %copy-start = (s32[3,2]{0,1:T(2,128)S(1)}, s32[3,2]{0,1:T(2,128)}, u32[]{:S(2)}) copy-start(s32[3,2]{0,1:T(2,128)} %param.6) | copy-start | bytes 76
  6.5 489.3 %all-reduce.3.cloned.1.call-start = ((), (), s32[]{:S(2)}) async-start(), calls=%async_computation | async-start | bytes 50331648
  22.9 14.0 %copy-start.2 = (s32[3]{0:T(128)S(1)}, s32[3]{0:T(128)}, u32[]{:S(2)}) copy-start(s32[3]{0:T(128)} %constant.152) | copy-start | bytes 40
  22.9 15.3 %copy-start.3 = (s32[48]{0:T(128)S(1)}, s32[48]{0:T(128)}, u32[]{:S(2)}) copy-start(s32[48]{0:T(128)} %param.5) | copy-start | bytes 580
  29.4 42.9 %collective-permute-start = (bf16[48,2,128,128]{3,2,0,1:T(8,128)(2,1)S(1)}, bf16[48,2,128,128]{3,2,0,1:T(8,128)(2,1)}, u32[]{:S(2)}, u32[]{:S(2)}) collective-permute-start(bf16[48,2,128,128]{3,2,0,1:T(8,128)(2,1)S(1)} %fusion.5), channel_id=1, source_target_pairs={{0,1},{1,2},{2,3},{3,4},{4,5},{5,6},{6,7},{8,9},{9,10},{10,11},{11... | collective-permute-start | bytes 9437192 | tf_op jit(solution)/shard_map/ppermute | solution.py:22
  34.3 38.7 %collective-permute-start.1 = (bf16[48,2,128,128]{3,2,0,1:T(8,128)(2,1)S(1)}, bf16[48,2,128,128]{3,2,0,1:T(8,128)(2,1)}, u32[]{:S(2)}, u32[]{:S(2)}) collective-permute-start(bf16[48,2,128,128]{3,2,0,1:T(8,128)(2,1)S(1)} %fusion.5), channel_id=1, source_target_pairs={{1,0},{2,1},{3,2},{4,3},{5,4},{6,5},{7,6},{9,8},{10,9},{11,10},{12... | collective-permute-start | bytes 9437192 | tf_op jit(solution)/shard_map/ppermute | solution.py:23
  188.2 0.7 copy-start.4
  188.2 310.9 %copy-start.1 = (s32[3,2]{0,1:T(2,128)S(1)}, s32[3,2]{0,1:T(2,128)}, u32[]{:S(2)}) copy-start(s32[3,2]{0,1:T(2,128)} %param.6) | copy-start | bytes 76
Sparse Core Ops, SparseCore 0:
  188.3 307.4 all-reduce.2
where the time goes:
time: 507 us; the launch traced here: 506 us
  waiting for transfers between devices  306 us (60%)
  local copies, waits for them, and re-layouts  79.4 us (16%)
  other arithmetic  49.3 us (10%)
  blocking collectives  33.7 us (7%)
  matrix products  15.5 us (3%)
  between operations  14.9 us (3%)
  starting transfers between devices  6.85 us (1%)
    unnamed x2, waiting for transfers between devices  306 us
    psum x1, blocking collectives, on_device(): sizes = lax.psum(jnp.sum(own_hot, axis=0), 'win')  33.7 us
    transpose x1, local copies, waits for them, and re-layouts, cross_spectrum(): jnp.einsum('qpwcf,pwdf->cqfd', left_both, right_both, preferred_element_t...  24.8 us
    mul x1, other arithmetic, on_device(): stacked = stacked * live_mask[:, None, None, None]  17.7 us
    gather x2, local copies, waits for them, and re-layouts, slot_cross(): lax.dynamic_index_in_dim(extended, pair_blocks[slot_index, 0] - first_loc...  14.3 us
    unnamed x13, local copies, waits for them, and re-layouts  13.7 us
    dot_general x1, matrix products, cross_spectrum(): jnp.einsum('qpwcf,pwdf->cqfd', left_both, right_both, preferred_element_t...  12.1 us
  transfers between devices with their start and end apart: 3, of which 2 were waited for; matrix products, arithmetic and copies ran while one was open for 0% of the time, Pallas kernels for 0%

commit v1 on v0

--- a/solution.py
+++ b/solution.py
@@ -10,6 +10,7 @@
 NFFT = 4096
 F0 = 64
 LAGS = 64
+SEG_MOST = 16
 
 
 def padded(value, sides, width):
@@ -47,7 +48,21 @@
     return jnp.concatenate([jnp.cos(phases), -jnp.sin(phases)], axis=0) * norm_scale
 
 
-def cross_spectrum(first_block, second_block, weight):
+def window_weight(segment_ids):
+    count = lax.axis_size("win")
+    length = segment_ids.shape[0]
+    up = [(i, i + 1) for i in range(count - 1)]
+    down = [(j, i) for i, j in up]
+    shifted = segment_ids + 1
+    before = lax.ppermute(shifted[length - SEG_MOST:], "win", up) - 1
+    after = lax.ppermute(shifted[:SEG_MOST], "win", down) - 1
+    extended = jnp.concatenate([before, segment_ids, after])
+    same = (segment_ids[:, None] == extended[None, :]).astype(jnp.float32)
+    sizes = jnp.sum(same, axis=1)
+    return 1.0 / sizes
+
+
+def slot_corr(first_block, second_block, weight, basis):
     left = (first_block.astype(jnp.float32) * weight[:, None, None]).astype(jnp.bfloat16)
     left_real, left_imag = (left[..., :FB], left[..., FB:])
     right_real, right_imag = (second_block[..., :FB], second_block[..., FB:])
@@ -56,39 +71,38 @@
     cross = jnp.einsum(
         "qpwcf,pwdf->cqfd", left_both, right_both, preferred_element_type=jnp.float32
     )
-    return cross.reshape(cross.shape[0], 2 * FB, cross.shape[3])
+    cross = cross.reshape(cross.shape[0], 2 * FB, cross.shape[3])
+    return jnp.einsum("cgd,gl->cld", cross, basis, precision=lax.Precision.HIGHEST)
 
 
 def on_device(spectra, segment_ids, pair_blocks, pair_count):
     whitened = whiten(spectra)
-    window_count = segment_ids.shape[0]
-    segment_total = lax.axis_size("win") * window_count // 8
-    labels = jnp.arange(segment_total, dtype=jnp.int32)
-    own_hot = (segment_ids[:, None] == labels[None, :]).astype(jnp.float32)
-    sizes = lax.psum(jnp.sum(own_hot, axis=0), "win")
-    weight = 1.0 / jnp.dot(own_hot, sizes, precision=lax.Precision.HIGHEST)
+    weight = window_weight(segment_ids)
     block_count = whitened.shape[1]
     extended = padded(whitened, (("tile", 1),), block_count)
     first_local = lax.axis_index("tile") * block_count - block_count
     basis = lag_table()
     slot_total = pair_blocks.shape[0]
     live_count = pair_count[0]
+    win_count = lax.axis_size("win")
 
-    def slot_cross(slot_index):
+    def one_slot(slot_index):
         first_block = lax.dynamic_index_in_dim(
             extended, pair_blocks[slot_index, 0] - first_local, 1, keepdims=False
         )
         second_block = lax.dynamic_index_in_dim(
             extended, pair_blocks[slot_index, 1] - first_local, 1, keepdims=False
         )
-        return cross_spectrum(first_block, second_block, weight)
+        corr = slot_corr(first_block, second_block, weight, basis)
+        live = (slot_index < live_count).astype(jnp.float32)
+        return corr * live
 
     slot_numbers = jnp.arange(slot_total, dtype=jnp.int32)
-    stacked = jax.vmap(slot_cross)(slot_numbers)
-    live_mask = (slot_numbers < live_count).astype(jnp.float32)
-    stacked = stacked * live_mask[:, None, None, None]
-    share = lax.psum_scatter(stacked, "win", scatter_dimension=1, tiled=True)
-    return jnp.einsum("pcgd,gl->pcld", share, basis, precision=lax.Precision.HIGHEST)
+    stacked = jax.vmap(one_slot)(slot_numbers)
+    channels = stacked.shape[1]
+    grouped = stacked.reshape(slot_total, win_count, channels // win_count, LAGS, -1)
+    grouped = jnp.moveaxis(grouped, 1, 0)
+    return lax.psum_scatter(grouped, "win", scatter_dimension=0, tiled=False)
 
 
 def solution(mesh):

time: 507 us -> 305 us (0.60)
  waiting for transfers between devices: 306 us -> 125 us
  blocking collectives: 33.7 us -> 0 us
  other arithmetic: 49.3 us -> 31.7 us
  matrix products: 15.5 us -> 31.2 us
  local copies, waits for them, and re-layouts: 79.4 us -> 89.9 us
  starting transfers between devices: 6.85 us -> 12.3 us
    unnamed x2, waiting for transfers between devices: 306 us -> 96 us
    psum x1 -> x0, blocking collectives: 33.7 us -> none  [on_device(): sizes = lax.psum(jnp.sum(own_hot, axis=0), 'win')]
    ppermute x1, waiting for transfers between devices: 0.01 us -> 24.1 us  [padded(): before = lax.ppermute(last, axis, up)]
    mul x1 -> x0, other arithmetic: 17.7 us -> none  [on_device(): stacked = stacked * live_mask[:, None, None, None]]
    dot_general x3 -> x2, matrix products: 15.5 us -> 31.2 us  [the longest x1 19 us: slot_corr(): jnp.einsum('cgd,gl->cld', cross, basis, precision=lax.Precision.HIGHEST)]
    reshape x0 -> x1, local copies, waits for them, and re-layouts: none -> 11.8 us  [on_device(): stacked.reshape(slot_total, win_count, channels // win_count, LAGS, -1)]
    ppermute x0 -> x2, starting transfers between devices: none -> 5.45 us  [the longest x1 4.17 us: window_weight(): before = lax.ppermute(shifted[length - SEG_MOST:], 'win', up) - 1]
    unnamed x13 -> x10, local copies, waits for them, and re-layouts: 13.7 us -> 12.4 us
  transfers between devices with their start and end apart: 3 -> 5, of which waited for: 2 -> 3; matrix products, arithmetic and copies ran while one was open for 0% -> 1% of each run, Pallas kernels for 0% -> 0%
where the time goes in v1:
time: 305 us; the launch traced here: 304 us
  waiting for transfers between devices  125 us (41%)
  local copies, waits for them, and re-layouts  89.9 us (29%)
  other arithmetic  31.7 us (10%)
  matrix products  31.2 us (10%)
  between operations  14.2 us (5%)
  starting transfers between devices  12.3 us (4%)
    unnamed x2, waiting for transfers between devices  96 us
    transpose x1, local copies, waits for them, and re-layouts, slot_corr(): jnp.einsum('qpwcf,pwdf->cqfd', left_both, right_both, preferred_element_t...  24.9 us
    ppermute x1, waiting for transfers between devices, padded(): before = lax.ppermute(last, axis, up)  24.1 us
    dot_general x1, matrix products, slot_corr(): jnp.einsum('cgd,gl->cld', cross, basis, precision=lax.Precision.HIGHEST)  19 us
    gather x2, local copies, waits for them, and re-layouts, one_slot(): lax.dynamic_index_in_dim(extended, pair_blocks[slot_index, 0] - first_loc...  14.2 us
    unnamed x10, local copies, waits for them, and re-layouts  12.4 us
    dot_general x1, matrix products, slot_corr(): jnp.einsum('qpwcf,pwdf->cqfd', left_both, right_both, preferred_element_t...  12.1 us
    reshape x1, local copies, waits for them, and re-layouts, on_device(): stacked.reshape(slot_total, win_count, channels // win_count, LAGS, -1)  11.8 us
  transfers between devices with their start and end apart: 5, of which 3 were waited for; matrix products, arithmetic and copies ran while one was open for 1% of the time, Pallas kernels for 0%

profile of v1, /device:TPU:1, one launch (start us, length us, event | category | flops | bytes accessed | tf_op | source)
XLA Modules:
  0.0 304.0 jit_solution(13313576120649859388)
XLA Ops:
  6.5 2.7 copy_convert_fusion
  9.3 4.4 %fusion.4 = f32[48,2,128,64]{3,2,0,1:T(8,128)} fusion(f32[48,2,128,128]{3,2,0,1:T(8,128)S(1)} %copy_convert_fusion), kind=kLoop, calls=%fused_computation.13 | loop fusion | flops 2359296 | bytes 9437184 | tf_op jit(solution)/shard_map/add | solution.py:33
  13.6 4.4 %copy.35 = f32[48,2,128,64]{2,3,1,0:T(8,128)S(1)} copy(f32[48,2,128,64]{3,2,0,1:T(8,128)} %fusion.4) | data formatting | bytes 6291456 | tf_op jit(solution)/shard_map/add | solution.py:33
  18.0 0.6 bitcast_reduce_fusion
  18.7 0.2 broadcast_in_dim.4
  18.9 4.1 %copy.36 = f32[48,2,128,64]{3,2,0,1:T(8,128)} copy(f32[48,2,128,64]{2,3,1,0:T(8,128)S(1)} %bitcast.59) | data formatting | bytes 6291456 | tf_op jit(solution)/shard_map/reshape | solution.py:37
  23.0 6.4 %fusion.5 = bf16[48,2,128,128]{3,2,0,1:T(8,128)(2,1)S(1)} fusion(f32[48,2,128,64]{3,2,0,1:T(8,128)} %copy.36, bf16[48,2,128,128]{3,2,1,0:T(8,128)(2,1)} %param.4), kind=kLoop, calls=%fused_computation.16 | loop fusion | flops 6291456 | bytes 9437184 | tf_op jit(solution)/shard_map/convert_element_type | solution.py:39
  29.4 4.9 %collective-permute-start = (bf16[48,2,128,128]{3,2,0,1:T(8,128)(2,1)S(1)}, bf16[48,2,128,128]{3,2,0,1:T(8,128)(2,1)}, u32[]{:S(2)}, u32[]{:S(2)}) collective-permute-start(bf16[48,2,128,128]{3,2,0,1:T(8,128)(2,1)S(1)} %fusion.5), channel_id=1, source_target_pairs={{0,1},{1,2},{2,3},{3,4},{4,5},{5,6},{6,7},{8,9},{9,10},{10,11},{11... | collective-permute-start | bytes 9437192 | tf_op jit(solution)/shard_map/ppermute | solution.py:23
  34.3 1.9 collective-permute-start.1
  36.4 1.3 collective-permute-start.3
  37.7 4.2 %collective-permute-start.2 = (s32[16]{0:T(128)S(1)}, s32[16]{0:T(128)S(1)}, u32[]{:S(2)}, u32[]{:S(2)}) collective-permute-start(s32[16]{0:T(128)S(1)} %get-tuple-element.13), channel_id=1, source_target_pairs={{0,8},{8,16},{16,24},{24,32},{32,40},{40,48},{48,56},{56,64},{64,7... | collective-permute-start | bytes 200 | tf_op jit(solution)/shard_map/ppermute | solution.py:57
  41.9 0.7 gather_fusion.2
  42.5 0.7 gather_fusion
  43.9 0.2 fusion.16
  44.2 0.2 convert_reduce_fusion
  44.4 24.1 %collective-permute-done = bf16[48,2,128,128]{3,2,0,1:T(8,128)(2,1)} collective-permute-done((bf16[48,2,128,128]{3,2,0,1:T(8,128)(2,1)S(1)}, bf16[48,2,128,128]{3,2,0,1:T(8,128)(2,1)}, u32[]{:S(2)}, u32[]{:S(2)}) %collective-permute-start) | collective-permute-done | bytes 3145760 | tf_op jit(solution)/shard_map/ppermute | solution.py:23
  68.5 4.5 %collective-permute-done.1 = bf16[48,2,128,128]{3,2,0,1:T(8,128)(2,1)} collective-permute-done((bf16[48,2,128,128]{3,2,0,1:T(8,128)(2,1)S(1)}, bf16[48,2,128,128]{3,2,0,1:T(8,128)(2,1)}, u32[]{:S(2)}, u32[]{:S(2)}) %collective-permute-start.1) | collective-permute-done | bytes 3145760 | tf_op jit(solution)/shard_map/ppermute | solution.py:24
  73.0 7.7 %pad_maximum_fusion = bf16[48,6,128,128]{3,2,0,1:T(8,128)(2,1)} fusion(bf16[48,2,128,128]{3,2,0,1:T(8,128)(2,1)} %collective-permute-done.1, bf16[48,2,128,128]{3,2,0,1:T(8,128)(2,1)S(1)} %fusion.5, bf16[48,2,128,128]{3,2,0,1:T(8,128)(2,1)} %collective-permute-done), kind=kLoop, calls=%fused_computation.6 | loop fusion | flops 9437184 | bytes 18874368 | tf_op jit(solution)/shard_map/concatenate | solution.py:25
  80.8 7.3 %gather_fusion.3 = bf16[3,48,128,128]{3,2,1,0:T(8,128)(2,1)} fusion(bf16[48,6,128,128]{3,2,0,1:T(8,128)(2,1)} %pad_maximum_fusion, s32[3]{0:T(128)S(1)} %get-tuple-element.16), kind=kCustom, calls=%fused_computation.3 | custom fusion | bytes 9437232 | tf_op jit(solution)/shard_map/vmap(jit(dynamic_index_in_dim))/gather | solution.py:90
  88.0 6.9 %copy.40 = bf16[3,48,128,128]{2,1,3,0:T(8,128)(2,1)} copy(bf16[3,48,128,128]{3,2,1,0:T(8,128)(2,1)} %gather_fusion.3) | data formatting | bytes 9437184 | tf_op jit(solution)/shard_map/vmap(jit(dynamic_index_in_dim))/gather | solution.py:90
  95.0 3.3 %fusion.3 = bf16[3,48,128,128]{2,1,3,0:T(8,128)(2,1)S(1)} fusion(bf16[3,48,128,128]{2,1,3,0:T(8,128)(2,1)} %copy.40, f32[48]{0:T(128)S(1)} %broadcast_divide_fusion), kind=kLoop, calls=%fused_computation.11 | loop fusion | flops 7077888 | bytes 9437376 | tf_op jit(solution)/shard_map/vmap()/convert_element_type | solution.py:66
  98.3 3.2 %slice_bitcast_fusion.2 = (bf16[1,3,48,128,64]{3,2,4,1,0:T(8,128)(2,1)S(1)}, bf16[1,3,48,128,64]{3,2,0,4,1:T(8,128)(2,1)}, bf16[1,3,48,128,64]{3,2,0,4,1:T(8,128)(2,1)}, bf16[1,3,48,128,64]{3,2,4,1,0:T(8,128)(2,1)}) fusion(bf16[3,48,128,128]{2,1,3,0:T(8,128)(2,1)S(1)} %fusion.3), kind=kLoop, calls=%fused_computation.28 | loop fusion | flops 1179648 | bytes 14155776 | tf_op jit(solution)/shard_map/vmap()/stack | solution.py:69
  101.5 7.3 %gather_fusion.1 = bf16[3,48,128,128]{3,2,1,0:T(8,128)(2,1)} fusion(bf16[48,6,128,128]{3,2,0,1:T(8,128)(2,1)} %pad_maximum_fusion, s32[3]{0:T(128)S(1)} %get-tuple-element.15), kind=kCustom, calls=%fused_computation.1 | custom fusion | bytes 9437232 | tf_op jit(solution)/shard_map/vmap(jit(dynamic_index_in_dim))/gather | solution.py:93
  108.8 9.3 %fusion.26 = (bf16[3,48,128,64]{3,2,1,0:T(8,128)(2,1)}, bf16[3,48,128,64]{3,2,1,0:T(8,128)(2,1)}) fusion(bf16[3,48,128,128]{3,2,1,0:T(8,128)(2,1)} %gather_fusion.1), kind=kLoop, calls=%fused_computation.65 | loop fusion | bytes 9437184 | tf_op jit(solution)/shard_map/vmap()/slice | solution.py:68
  118.1 6.2 %copy.48 = bf16[3,48,128,64]{2,1,3,0:T(8,128)(2,1)} copy(bf16[3,48,128,64]{3,2,1,0:T(8,128)(2,1)} %get-tuple-element.5) | data formatting | bytes 4718592
  124.3 6.2 %copy.49 = bf16[3,48,128,64]{2,1,3,0:T(8,128)(2,1)} copy(bf16[3,48,128,64]{3,2,1,0:T(8,128)(2,1)} %get-tuple-element.6) | data formatting | bytes 4718592
  130.5 2.8 maximum_bitcast_fusion.3
  133.3 12.1 %convolution_bitcast_fusion = f32[3,128,2,64,128]{1,4,2,3,0:T(8,128)} fusion(bf16[1,2,3,48,128,64]{4,3,1,0,5,2:T(8,128)(2,1)S(1)} %maximum_bitcast_fusion.3, bf16[1,3,48,128,64]{3,2,0,4,1:T(8,128)(2,1)} %bitcast.61, bf16[1,3,48,128,64]{3,2,0,4,1:T(8,128)(2,1)} %bitcast.60, bf16[1,3,48,128,64]{3,2,4,1,0:T(8,128)(2,1)} %get-tuple-element.10, ...), kind=kOutput, calls=%fused_computation.5 | convolution fusion | flops 1238630400 | bytes 39321600 | tf_op jit(solution)/shard_map/vmap(qpwcf,pwdf->cqfd)/dot_general | solution.py:71
  145.4 24.9 %copy.43 = f32[3,128,2,64,128]{4,3,2,1,0:T(8,128)} copy(f32[3,128,2,64,128]{1,4,2,3,0:T(8,128)} %convolution_bitcast_fusion) | data formatting | bytes 50331648 | tf_op jit(solution)/shard_map/vmap(qpwcf,pwdf->cqfd)/transpose | solution.py:71
  170.3 19.0 %broadcast_multiply_fusion = f32[64,3,128,128]{3,0,2,1:T(8,128)} fusion(f32[3]{0:T(128)S(1)} %compare_convert_fusion, f32[3,128,128,128]{3,2,1,0:T(8,128)} %bitcast.56, f32[64,64]{0,1:T(8,128)S(1)} %get-tuple-element.12, f32[64,64]{0,1:T(8,128)S(1)} %get-tuple-element.11), kind=kOutput, calls=%fused_computation.17 | convolution fusion | flops 4835000320 | bytes 37781516 | tf_op jit(solution)/shard_map/vmap(cgd,gl->cld)/dot_general | solution.py:75
  189.3 11.8 %copy.57 = f32[3,16,8,64,128]{4,3,2,0,1:T(8,128)} copy(f32[3,16,8,64,128]{4,3,2,1,0:T(8,128)} %bitcast.58) | data formatting | bytes 25165824 | tf_op jit(solution)/shard_map/reshape | solution.py:103
  201.1 96.0 %reduce-scatter.4.cloned.1.call-done = f32[1,3,8,64,128]{4,3,2,1,0:T(8,128)} async-done(((f32[16,3,8,64,128]{4,3,2,1,0:T(8,128)}), f32[1,3,8,64,128]{4,3,2,1,0:T(8,128)}) %reduce-scatter.4.cloned.1.call-update) | async-done | bytes 786448
  (23 shorter events, 0.3 us)
Async XLA Ops:
  6.5 35.3 %copy-start = (s32[3,2]{0,1:T(2,128)S(1)}, s32[3,2]{0,1:T(2,128)}, u32[]{:S(2)}) copy-start(s32[3,2]{0,1:T(2,128)} %param.6) | copy-start | bytes 76
  6.5 290.6 %reduce-scatter.4.cloned.1.call-start = ((), (), s32[]{:S(2)}) async-start(), calls=%async_computation.1 | async-start | bytes 13369344
  23.0 13.3 %copy-start.3 = (s32[48]{0:T(128)S(1)}, s32[48]{0:T(128)}, u32[]{:S(2)}) copy-start(s32[48]{0:T(128)} %param.5) | copy-start | bytes 580
  23.0 19.5 %copy-start.2 = (s32[3]{0:T(128)S(1)}, s32[3]{0:T(128)}, u32[]{:S(2)}) copy-start(s32[3]{0:T(128)} %constant.158) | copy-start | bytes 40
  29.4 39.1 %collective-permute-start = (bf16[48,2,128,128]{3,2,0,1:T(8,128)(2,1)S(1)}, bf16[48,2,128,128]{3,2,0,1:T(8,128)(2,1)}, u32[]{:S(2)}, u32[]{:S(2)}) collective-permute-start(bf16[48,2,128,128]{3,2,0,1:T(8,128)(2,1)S(1)} %fusion.5), channel_id=1, source_target_pairs={{0,1},{1,2},{2,3},{3,4},{4,5},{5,6},{6,7},{8,9},{9,10},{10,11},{11... | collective-permute-start | bytes 9437192 | tf_op jit(solution)/shard_map/ppermute | solution.py:23
  34.3 38.7 %collective-permute-start.1 = (bf16[48,2,128,128]{3,2,0,1:T(8,128)(2,1)S(1)}, bf16[48,2,128,128]{3,2,0,1:T(8,128)(2,1)}, u32[]{:S(2)}, u32[]{:S(2)}) collective-permute-start(bf16[48,2,128,128]{3,2,0,1:T(8,128)(2,1)S(1)} %fusion.5), channel_id=1, source_target_pairs={{1,0},{2,1},{3,2},{4,3},{5,4},{6,5},{7,6},{9,8},{10,9},{11,10},{12... | collective-permute-start | bytes 9437192 | tf_op jit(solution)/shard_map/ppermute | solution.py:24
  36.4 7.7 %collective-permute-start.3 = (s32[16]{0:T(128)S(1)}, s32[16]{0:T(128)S(1)}, u32[]{:S(2)}, u32[]{:S(2)}) collective-permute-start(s32[16]{0:T(128)S(1)} %get-tuple-element.14), channel_id=1, source_target_pairs={{8,0},{16,8},{24,16},{32,24},{40,32},{48,40},{56,48},{64,56},{72,6... | collective-permute-start | bytes 200 | tf_op jit(solution)/shard_map/ppermute | solution.py:58
  37.7 6.5 %collective-permute-start.2 = (s32[16]{0:T(128)S(1)}, s32[16]{0:T(128)S(1)}, u32[]{:S(2)}, u32[]{:S(2)}) collective-permute-start(s32[16]{0:T(128)S(1)} %get-tuple-element.13), channel_id=1, source_target_pairs={{0,8},{8,16},{16,24},{24,32},{32,40},{40,48},{48,56},{56,64},{64,7... | collective-permute-start | bytes 200 | tf_op jit(solution)/shard_map/ppermute | solution.py:57
  201.1 96.1 %copy-start.1 = (s32[3,2]{0,1:T(2,128)S(1)}, s32[3,2]{0,1:T(2,128)}, u32[]{:S(2)}) copy-start(s32[3,2]{0,1:T(2,128)} %param.6) | copy-start | bytes 76
Sparse Core Ops, SparseCore 0:
  201.2 95.8 reduce-scatter.3

commit v2 on v1

v2 whole, which is shorter than its diff:
```python
import functools
import math

import jax
import jax.numpy as jnp
from jax import lax
from jax.experimental import pallas as pl
from jax.experimental.pallas import tpu as pltpu
from jax.sharding import PartitionSpec as P

FB = 64
SUB = 32
NFFT = 4096
F0 = 64
LAGS = 64
SEG_MOST = 16


def padded(value, sides, width):
    for axis, dim in sides:
        count, length = (lax.axis_size(axis), value.shape[dim])
        up = [(i, (i + 1) % count) for i in range(count - 1)]
        down = [(j, i) for i, j in up]
        last = lax.slice_in_dim(value, length - width, length, axis=dim)
        initial = lax.slice_in_dim(value, 0, width, axis=dim)
        before = lax.ppermute(last, axis, up)
        after = lax.ppermute(initial, axis, down)
        value = jnp.concatenate([before, value, after], axis=dim)
    return value


def whiten_transposed(spectra):
    values = spectra.astype(jnp.float32)
    real_part = values[..., :FB]
    imag_part = values[..., FB:]
    power_sum = real_part * real_part + imag_part * imag_part
    band_power = (
        jnp.mean(power_sum.reshape(power_sum.shape[:-1] + (FB // SUB, SUB)), axis=-1) + 1e-06
    )
    scales = jnp.repeat(1.0 / jnp.sqrt(band_power), SUB, axis=-1)
    both_scales = jnp.concatenate([scales, scales], axis=-1)
    whitened = (values * both_scales).astype(jnp.bfloat16)
    return jnp.transpose(whitened, (1, 3, 0, 2))


def lag_table():
    bins = jnp.arange(FB, dtype=jnp.int32) + F0
    shifts = jnp.arange(LAGS, dtype=jnp.int32) - LAGS // 2
    products = jnp.mod(bins[:, None] * shifts[None, :], NFFT)
    phases = products.astype(jnp.float32) * (2.0 * math.pi / NFFT)
    norm_scale = 1.0 / math.sqrt(FB)
    return jnp.concatenate([jnp.cos(phases), -jnp.sin(phases)], axis=0) * norm_scale


def window_weight(segment_ids):
    count = lax.axis_size("win")
    length = segment_ids.shape[0]
    up = [(i, i + 1) for i in range(count - 1)]
    down = [(j, i) for i, j in up]
    shifted = segment_ids + 1
    before = lax.ppermute(shifted[length - SEG_MOST:], "win", up) - 1
    after = lax.ppermute(shifted[:SEG_MOST], "win", down) - 1
    extended = jnp.concatenate([before, segment_ids, after])
    same = (segment_ids[:, None] == extended[None, :]).astype(jnp.float32)
    sizes = jnp.sum(same, axis=1)
    return 1.0 / sizes


def corr_kernel(index_ref, a_ref, b_ref, w_ref, basis_ref, o_ref, x_ref, *, groups):
    channels = a_ref.shape[2]
    weight = w_ref[...]
    dims = (((0,), (0,)), ((), ()))

    def cross_step(k, carry):
        a_real = (a_ref[k].astype(jnp.float32) * weight).astype(jnp.bfloat16)
        a_imag = (a_ref[k + FB].astype(jnp.float32) * weight).astype(jnp.bfloat16)
        right = jnp.concatenate([b_ref[k], b_ref[k + FB]], axis=0)
        first = jnp.concatenate([a_real, a_imag], axis=0)
        second = jnp.concatenate([a_imag, -a_real], axis=0)
        base = pl.multiple_of(k * 2 * channels, 2 * channels)
        x_ref[pl.ds(base, channels), :] = lax.dot_general(
            first, right, dims, preferred_element_type=jnp.float32
        )
        x_ref[pl.ds(base + channels, channels), :] = lax.dot_general(
            second, right, dims, preferred_element_type=jnp.float32
        )
        return carry

    lax.fori_loop(0, FB, cross_step, 0)
    live = (index_ref[2] > 0).astype(jnp.float32)
    basis = basis_ref[...]
    rows = channels // groups

    def lag_step(c, carry):
        real_rows = x_ref[pl.ds(c, FB, stride=2 * channels), :]
        imag_rows = x_ref[pl.ds(c + channels, FB, stride=2 * channels), :]
        both = jnp.concatenate([real_rows, imag_rows], axis=0)
        lagged = jnp.dot(
            basis, both, precision=lax.Precision.HIGHEST, preferred_element_type=jnp.float32
        )
        o_ref[c // rows, c % rows] = lagged * live
        return carry

    lax.fori_loop(0, channels, lag_step, 0)


def slot_corr(index, extended, weight, basis_t, groups):
    blocks, bins, windows, channels = extended.shape
    kernel = functools.partial(corr_kernel, groups=groups)
    spec = pl.BlockSpec((None, bins, windows, channels), lambda i, ref: (ref[0], 0, 0, 0))
    second_spec = pl.BlockSpec((None, bins, windows, channels), lambda i, ref: (ref[1], 0, 0, 0))
    grid_spec = pltpu.PrefetchScalarGridSpec(
        num_scalar_prefetch=1,
        grid=(1,),
        in_specs=[
            spec,
            second_spec,
            pl.BlockSpec((windows, 1), lambda i, ref: (0, 0)),
            pl.BlockSpec((LAGS, 2 * FB), lambda i, ref: (0, 0)),
        ],
        out_specs=pl.BlockSpec(
            (groups, channels // groups, LAGS, channels), lambda i, ref: (0, 0, 0, 0)
        ),
        scratch_shapes=[pltpu.VMEM((FB * 2 * channels, channels), jnp.float32)],
    )
    return pl.pallas_call(
        kernel,
        grid_spec=grid_spec,
        out_shape=jax.ShapeDtypeStruct(
            (groups, channels // groups, LAGS, channels), jnp.float32
        ),
        compiler_params=pltpu.CompilerParams(vmem_limit_bytes=48 * 1024 * 1024),
    )(index, extended, extended, weight[:, None], basis_t)


def on_device(spectra, segment_ids, pair_blocks, pair_count):
    weight = window_weight(segment_ids)
    whitened = whiten_transposed(spectra)
    block_count = whitened.shape[0]
    extended = padded(whitened, (("tile", 0),), block_count)
    first_local = lax.axis_index("tile") * block_count - block_count
    basis_t = jnp.transpose(lag_table())
    slot_total = pair_blocks.shape[0]
    live_count = pair_count[0]
    win_count = lax.axis_size("win")
    local = jnp.clip(pair_blocks - first_local, 0, extended.shape[0] - 1)

    shares = []
    for slot in range(slot_total):
        index = jnp.stack(
            [local[slot, 0], local[slot, 1], (slot < live_count).astype(jnp.int32)]
        )
        corr = slot_corr(index, extended, weight, basis_t, win_count)
        shares.append(lax.psum_scatter(corr, "win", scatter_dimension=0, tiled=False))
    return jnp.stack(shares)


def solution(mesh):
    return jax.shard_map(
        on_device,
        mesh=mesh,
        in_specs=(P("win", "tile", None, None), P("win"), P("tile", None), P("tile")),
        out_specs=P("tile", "win", None, None),
        check_vma=False,
    )
```

time: 305 us -> 373 us (1.22)
  Pallas kernels: 0 us -> 151 us
  local copies, waits for them, and re-layouts: 89.9 us -> 10.7 us
  waiting for transfers between devices: 125 us -> 162 us
  matrix products: 31.2 us -> 0 us
  other arithmetic: 31.7 us -> 21.5 us
    pallas_call x0 -> x3, Pallas kernels: none -> 151 us  [slot_corr(): pl.pallas_call(kernel, grid_spec=grid_spec, out_shape=jax.ShapeDtypeStruc...]
    unnamed x2 -> x6, waiting for transfers between devices: 96 us -> 134 us
    dot_general x2 -> x0, matrix products: 31.2 us -> none  [the longest x1 19 us: slot_corr(): jnp.einsum('cgd,gl->cld', cross, basis, precision=lax.Precision.HIGHEST)]
    transpose x1 -> x0, local copies, waits for them, and re-layouts: 24.9 us -> none  [slot_corr(): jnp.einsum('qpwcf,pwdf->cqfd', left_both, right_both, preferred_element_t...]
    gather x5 -> x0, local copies, waits for them, and re-layouts: 22.8 us -> none  [the longest x2 14.2 us: one_slot(): lax.dynamic_index_in_dim(extended, pair_blocks[slot_index, 0] - first_loc...]
    reshape x2 -> x0, local copies, waits for them, and re-layouts: 15.9 us -> none  [the longest x1 11.8 us: on_device(): stacked.reshape(slot_total, win_count, channels // win_count, LAGS, -1)]
    convert_element_type x4 -> x1, other arithmetic: 12.5 us -> 0.49 us  [whiten_transposed(): values = spectra.astype(jnp.float32)]
    slice x1, local copies, waits for them, and re-layouts: 9.33 us -> 0.66 us  [on_device(): local[slot, 0]]
  transfers between devices with their start and end apart: 5 -> 7, of which waited for: 3 -> 4; matrix products, arithmetic and copies ran while one was open for 1% -> 1% of each run, Pallas kernels for 0% -> 27%
where the time goes in v2:
time: 373 us; the launch traced here: 371 us
  waiting for transfers between devices  162 us (43%)
  Pallas kernels  151 us (40%)
  other arithmetic  21.5 us (6%)
  between operations  14 us (4%)
  starting transfers between devices  12.2 us (3%)
  local copies, waits for them, and re-layouts  10.7 us (3%)
    pallas_call x3, Pallas kernels, slot_corr(): pl.pallas_call(kernel, grid_spec=grid_spec, out_shape=jax.ShapeDtypeStruc...  151 us
    unnamed x6, waiting for transfers between devices  134 us
    ppermute x1, waiting for transfers between devices, padded(): before = lax.ppermute(last, axis, up)  23.8 us
    unnamed x11, local copies, waits for them, and re-layouts  9.62 us
    concatenate x1, other arithmetic, padded(): value = jnp.concatenate([before, value, after], axis=dim)  7.72 us
  transfers between devices with their start and end apart: 7, of which 4 were waited for; matrix products, arithmetic and copies ran while one was open for 1% of the time, Pallas kernels for 27%

profile of v2, /device:TPU:1, one launch (start us, length us, event | category | flops | bytes accessed | tf_op | source)
XLA Modules:
  0.0 371.4 jit_solution(6331428323151037484)
XLA Ops:
  6.5 3.7 copy.13
  10.2 0.5 convert_element_type.27
  10.7 2.0 fusion.2
  12.8 2.0 reduce_sum.18
  14.8 0.2 broadcast_in_dim.2
  15.1 2.5 fusion.1
  17.6 4.9 %collective-permute-start = (bf16[2,128,48,128]{3,2,1,0:T(8,128)(2,1)}, bf16[2,128,48,128]{3,2,1,0:T(8,128)(2,1)S(1)}, u32[]{:S(2)}, u32[]{:S(2)}) collective-permute-start(bf16[2,128,48,128]{3,2,1,0:T(8,128)(2,1)} %fusion.1), channel_id=1, source_target_pairs={{0,1},{1,2},{2,3},{3,4},{4,5},{5,6},{6,7},{8,9},{9,10},{10,11},{11... | collective-permute-start | bytes 9437192 | tf_op jit(solution)/shard_map/ppermute | solution.py:26
  22.5 1.9 collective-permute-start.1
  24.4 0.1 fusion.9
  24.5 1.3 collective-permute-start.3
  25.8 4.0 %collective-permute-start.2 = (s32[16]{0:T(128)S(1)}, s32[16]{0:T(128)S(1)}, u32[]{:S(2)}, u32[]{:S(2)}) collective-permute-start(s32[16]{0:T(128)S(1)} %get-tuple-element.13), channel_id=1, source_target_pairs={{0,8},{8,16},{16,24},{24,32},{32,40},{40,48},{48,56},{56,64},{64,7... | collective-permute-start | bytes 200 | tf_op jit(solution)/shard_map/ppermute | solution.py:61
  30.5 0.7 fusion.8
  31.1 0.2 fusion.7
  31.3 0.1 fusion.6.basis_ref
  31.4 1.4 pad_add_fusion.index_ref
  32.8 0.1 pad_add_fusion.1
  32.9 0.2 convert_reduce_fusion
  33.1 0.1 copy.14.w_ref
  33.2 23.8 %collective-permute-done = bf16[2,128,48,128]{3,2,1,0:T(8,128)(2,1)S(1)} collective-permute-done((bf16[2,128,48,128]{3,2,1,0:T(8,128)(2,1)}, bf16[2,128,48,128]{3,2,1,0:T(8,128)(2,1)S(1)}, u32[]{:S(2)}, u32[]{:S(2)}) %collective-permute-start) | collective-permute-done | bytes 3145760 | tf_op jit(solution)/shard_map/ppermute | solution.py:26
  57.0 4.4 %collective-permute-done.1 = bf16[2,128,48,128]{3,2,1,0:T(8,128)(2,1)} collective-permute-done((bf16[2,128,48,128]{3,2,1,0:T(8,128)(2,1)}, bf16[2,128,48,128]{3,2,1,0:T(8,128)(2,1)}, u32[]{:S(2)}, u32[]{:S(2)}) %collective-permute-start.1) | collective-permute-done | bytes 3145760 | tf_op jit(solution)/shard_map/ppermute | solution.py:27
  61.4 7.7 %pad_maximum_fusion.a_ref.b_ref = bf16[6,128,48,128]{3,2,1,0:T(8,128)(2,1)} fusion(bf16[2,128,48,128]{3,2,1,0:T(8,128)(2,1)} %collective-permute-done.1, bf16[2,128,48,128]{3,2,1,0:T(8,128)(2,1)} %fusion.1, bf16[2,128,48,128]{3,2,1,0:T(8,128)(2,1)S(1)} %collective-permute-done), kind=kLoop, calls=%fused_computation | loop fusion | flops 9437184 | bytes 18874368 | tf_op jit(solution)/shard_map/concatenate | solution.py:28
  69.1 50.4 %shard_map.46 = f32[16,8,64,128]{3,2,1,0:T(8,128)S(1)} custom-call(s32[3]{0:T(128)S(1)} %pad_add_fusion.index_ref, bf16[6,128,48,128]{3,2,1,0:T(8,128)(2,1)} %pad_maximum_fusion.a_ref.b_ref, bf16[6,128,48,128]{3,2,1,0:T(8,128)(2,1)} %pad_maximum_fusion.a_ref.b_ref, f32[48,1]{1,0:T(8,128)S(1)} %copy.14.w_ref, f32[64,128]{1,0:T(8,128)S(1)} %fusion.6.basis_ref), custom_call_target="tpu_custom_call" | custom-call | tf_op jit(solution)/shard_map/pallas_call | solution.py:126
  119.5 2.1 copy-done
  121.6 1.3 pad_add_fusion.2.index_ref
  123.0 50.4 %shard_map.47 = f32[16,8,64,128]{3,2,1,0:T(8,128)S(1)} custom-call(s32[3]{0:T(128)S(1)} %pad_add_fusion.2.index_ref, bf16[6,128,48,128]{3,2,1,0:T(8,128)(2,1)} %pad_maximum_fusion.a_ref.b_ref, bf16[6,128,48,128]{3,2,1,0:T(8,128)(2,1)} %pad_maximum_fusion.a_ref.b_ref, f32[48,1]{1,0:T(8,128)S(1)} %copy.14.w_ref, f32[64,128]{1,0:T(8,128)S(1)} %fusion.6.basis_ref), custom_call_target="tpu_custom_call" | custom-call | tf_op jit(solution)/shard_map/pallas_call | solution.py:126
  173.4 1.9 copy-done.1
  175.4 1.4 pad_add_fusion.3.index_ref
  176.7 50.4 %shard_map.48 = f32[16,8,64,128]{3,2,1,0:T(8,128)S(1)} custom-call(s32[3]{0:T(128)S(1)} %pad_add_fusion.3.index_ref, bf16[6,128,48,128]{3,2,1,0:T(8,128)(2,1)} %pad_maximum_fusion.a_ref.b_ref, bf16[6,128,48,128]{3,2,1,0:T(8,128)(2,1)} %pad_maximum_fusion.a_ref.b_ref, f32[48,1]{1,0:T(8,128)S(1)} %copy.14.w_ref, f32[64,128]{1,0:T(8,128)S(1)} %fusion.6.basis_ref), custom_call_target="tpu_custom_call" | custom-call | tf_op jit(solution)/shard_map/pallas_call | solution.py:126
  227.1 1.9 copy-done.2
  229.1 52.8 %reduce-scatter.12.cloned.1.call-done = f32[1,8,64,128]{3,2,1,0:T(8,128)} async-done(((f32[16,8,64,128]{3,2,1,0:T(8,128)}), f32[1,8,64,128]{3,2,1,0:T(8,128)}) %reduce-scatter.12.cloned.1.call-update) | async-done | bytes 262160
  281.9 81.0 %reduce-scatter.14.cloned.1.call-done = f32[1,8,64,128]{3,2,1,0:T(8,128)} async-done(((f32[16,8,64,128]{3,2,1,0:T(8,128)}), f32[1,8,64,128]{3,2,1,0:T(8,128)}) %reduce-scatter.14.cloned.1.call-update) | async-done | bytes 262160
  362.8 2.1 pad_maximum_fusion.1
  (23 shorter events, 0.2 us)
Async XLA Ops:
  6.5 222.6 %reduce-scatter.10.cloned.1.call-start = ((), (), s32[]{:S(2)}) async-start(), calls=%async_computation.3 | async-start | bytes 4456448
  15.1 9.3 %copy-start.4 = (s32[48]{0:T(128)S(1)}, s32[48]{0:T(128)}, u32[]{:S(2)}) copy-start(s32[48]{0:T(128)} %param.5) | copy-start | bytes 580
  15.1 15.4 %copy-start.3 = (s32[3,2]{0,1:T(2,128)S(1)}, s32[3,2]{0,1:T(2,128)}, u32[]{:S(2)}) copy-start(s32[3,2]{0,1:T(2,128)} %param.6) | copy-start | bytes 76
  17.6 39.4 %collective-permute-start = (bf16[2,128,48,128]{3,2,1,0:T(8,128)(2,1)}, bf16[2,128,48,128]{3,2,1,0:T(8,128)(2,1)S(1)}, u32[]{:S(2)}, u32[]{:S(2)}) collective-permute-start(bf16[2,128,48,128]{3,2,1,0:T(8,128)(2,1)} %fusion.1), channel_id=1, source_target_pairs={{0,1},{1,2},{2,3},{3,4},{4,5},{5,6},{6,7},{8,9},{9,10},{10,11},{11... | collective-permute-start | bytes 9437192 | tf_op jit(solution)/shard_map/ppermute | solution.py:26
  22.5 38.9 %collective-permute-start.1 = (bf16[2,128,48,128]{3,2,1,0:T(8,128)(2,1)}, bf16[2,128,48,128]{3,2,1,0:T(8,128)(2,1)}, u32[]{:S(2)}, u32[]{:S(2)}) collective-permute-start(bf16[2,128,48,128]{3,2,1,0:T(8,128)(2,1)} %fusion.1), channel_id=1, source_target_pairs={{1,0},{2,1},{3,2},{4,3},{5,4},{6,5},{7,6},{9,8},{10,9},{11,10},{12... | collective-permute-start | bytes 9437192 | tf_op jit(solution)/shard_map/ppermute | solution.py:27
  24.5 8.3 %collective-permute-start.3 = (s32[16]{0:T(128)S(1)}, s32[16]{0:T(128)S(1)}, u32[]{:S(2)}, u32[]{:S(2)}) collective-permute-start(s32[16]{0:T(128)S(1)} %get-tuple-element.14), channel_id=1, source_target_pairs={{8,0},{16,8},{24,16},{32,24},{40,32},{48,40},{56,48},{64,56},{72,6... | collective-permute-start | bytes 200 | tf_op jit(solution)/shard_map/ppermute | solution.py:62
  25.8 7.0 %collective-permute-start.2 = (s32[16]{0:T(128)S(1)}, s32[16]{0:T(128)S(1)}, u32[]{:S(2)}, u32[]{:S(2)}) collective-permute-start(s32[16]{0:T(128)S(1)} %get-tuple-element.13), channel_id=1, source_target_pairs={{0,8},{8,16},{16,24},{24,32},{32,40},{40,48},{48,56},{56,64},{64,7... | collective-permute-start | bytes 200 | tf_op jit(solution)/shard_map/ppermute | solution.py:61
  119.5 2.1 copy-start
  121.6 160.3 %reduce-scatter.12.cloned.1.call-start = ((), (), s32[]{:S(2)}) async-start(), calls=%async_computation.4 | async-start | bytes 4456448
  173.4 1.9 copy-start.1
  175.3 187.5 %reduce-scatter.14.cloned.1.call-start = ((), (), s32[]{:S(2)}) async-start(), calls=%async_computation.5 | async-start | bytes 4456448
  227.1 1.9 copy-start.2
Sparse Core Ops, SparseCore 0:
  121.7 78.9 reduce-scatter.9
  204.0 77.7 reduce-scatter.11
  285.2 77.5 reduce-scatter.13

commit v3 on v1

v3 whole, which is shorter than its diff:
```python
import math
import jax
import jax.numpy as jnp
from jax import lax
from jax.experimental.layout import Layout, with_layout_constraint
from jax.sharding import PartitionSpec as P

FB = 64
SUB = 32
NFFT = 4096
F0 = 64
LAGS = 64
SEG_MOST = 16


def padded(value, sides, width):
    for axis, dim in sides:
        count, length = (lax.axis_size(axis), value.shape[dim])
        up = [(i, (i + 1) % count) for i in range(count - 1)]
        down = [(j, i) for i, j in up]
        last = lax.slice_in_dim(value, length - width, length, axis=dim)
        initial = lax.slice_in_dim(value, 0, width, axis=dim)
        before = lax.ppermute(last, axis, up)
        after = lax.ppermute(initial, axis, down)
        value = jnp.concatenate([before, value, after], axis=dim)
    return value


def whiten_transposed(spectra):
    values = spectra.astype(jnp.float32)
    real_part = values[..., :FB]
    imag_part = values[..., FB:]
    power_sum = real_part * real_part + imag_part * imag_part
    band_power = (
        jnp.mean(power_sum.reshape(power_sum.shape[:-1] + (FB // SUB, SUB)), axis=-1) + 1e-06
    )
    scales = jnp.repeat(1.0 / jnp.sqrt(band_power), SUB, axis=-1)
    both_scales = jnp.concatenate([scales, scales], axis=-1)
    whitened = (values * both_scales).astype(jnp.bfloat16)
    return jnp.transpose(whitened, (1, 3, 0, 2))


def lag_table():
    bins = jnp.arange(FB, dtype=jnp.int32) + F0
    shifts = jnp.arange(LAGS, dtype=jnp.int32) - LAGS // 2
    products = jnp.mod(bins[:, None] * shifts[None, :], NFFT)
    phases = products.astype(jnp.float32) * (2.0 * math.pi / NFFT)
    norm_scale = 1.0 / math.sqrt(FB)
    return jnp.concatenate([jnp.cos(phases), -jnp.sin(phases)], axis=0) * norm_scale


def window_weight(segment_ids):
    count = lax.axis_size("win")
    length = segment_ids.shape[0]
    up = [(i, i + 1) for i in range(count - 1)]
    down = [(j, i) for i, j in up]
    shifted = segment_ids + 1
    before = lax.ppermute(shifted[length - SEG_MOST:], "win", up) - 1
    after = lax.ppermute(shifted[:SEG_MOST], "win", down) - 1
    extended = jnp.concatenate([before, segment_ids, after])
    same = (segment_ids[:, None] == extended[None, :]).astype(jnp.float32)
    sizes = jnp.sum(same, axis=1)
    return 1.0 / sizes


def on_device(spectra, segment_ids, pair_blocks, pair_count):
    weight = window_weight(segment_ids)
    whitened = whiten_transposed(spectra)
    block_count = whitened.shape[0]
    extended = padded(whitened, (("tile", 0),), block_count)
    first_local = lax.axis_index("tile") * block_count - block_count
    basis = lag_table().reshape(2, FB, LAGS)
    slot_total = pair_blocks.shape[0]
    live_count = pair_count[0]
    win_count = lax.axis_size("win")
    local = jnp.clip(pair_blocks - first_local, 0, extended.shape[0] - 1)
    first = jnp.take(extended, local[:, 0], axis=0)
    second = jnp.take(extended, local[:, 1], axis=0)
    left = (first.astype(jnp.float32) * weight[None, None, :, None]).astype(jnp.bfloat16)
    left_real, left_imag = (left[:, :FB], left[:, FB:])
    right_real, right_imag = (second[:, :FB], second[:, FB:])
    left_both = jnp.stack([jnp.stack([left_real, left_imag]), jnp.stack([left_imag, -left_real])])
    right_both = jnp.stack([right_real, right_imag])
    cross = jnp.einsum(
        "qpskwc,pskwd->skqcd", left_both, right_both, preferred_element_type=jnp.float32
    )
    live = (jnp.arange(slot_total) < live_count).astype(jnp.float32)
    channels = cross.shape[3]
    cross = cross.reshape(slot_total, FB, 2, win_count, channels // win_count, channels)
    corr = jnp.einsum(
        "skqgcd,qkl->gsc" + "ld", cross, basis, precision=lax.Precision.HIGHEST
    )
    corr = corr * live[None, :, None, None, None]
    corr = with_layout_constraint(corr, Layout((0, 1, 2, 3, 4)))
    return lax.psum_scatter(corr, "win", scatter_dimension=0, tiled=False)


def solution(mesh):
    return jax.shard_map(
        on_device,
        mesh=mesh,
        in_specs=(P("win", "tile", None, None), P("win"), P("tile", None), P("tile")),
        out_specs=P("tile", "win", None, None),
        check_vma=False,
    )
```

time: 305 us -> 254 us (0.83)
  local copies, waits for them, and re-layouts: 89.9 us -> 23.3 us
  matrix products: 31.2 us -> 49.8 us
  other arithmetic: 31.7 us -> 27.6 us
    transpose x1 -> x0, local copies, waits for them, and re-layouts: 24.9 us -> none  [slot_corr(): jnp.einsum('qpwcf,pwdf->cqfd', left_both, right_both, preferred_element_t...]
    dot_general x2, matrix products: 31.2 us -> 49.8 us  [the longest x1 36.7 us: on_device(): jnp.einsum('skqgcd,qkl->gsc' + 'ld', cross, basis, precision=lax.Precisio...]
    reshape x2 -> x1, local copies, waits for them, and re-layouts: 15.9 us -> 1.82 us  [whiten_transposed(): scales = jnp.repeat(1.0 / jnp.sqrt(band_power), SUB, axis=-1)]
    slice x1 -> x0, local copies, waits for them, and re-layouts: 9.33 us -> none  [slot_corr(): right_real, right_imag = (second_block[..., :FB], second_block[..., FB:])]
    unnamed x10 -> x7, local copies, waits for them, and re-layouts: 12.4 us -> 3.7 us
    gather x5 -> x2, local copies, waits for them, and re-layouts: 22.8 us -> 14.4 us  [the longest x1 7.21 us: on_device(): second = jnp.take(extended, local[:, 1], axis=0)]
    convert_element_type x4 -> x3, other arithmetic: 12.5 us -> 4.11 us  [the longest x1 3.62 us: on_device(): (first.astype(jnp.float32) * weight[None, None, :, None]).astype(jnp.bflo...]
    add x1 -> x0, local copies, waits for them, and re-layouts: 4.39 us -> none  [whiten(): power_sum = real_part * real_part + imag_part * imag_part]
  transfers between devices with their start and end apart: 5 -> 5, of which waited for: 3 -> 3; matrix products, arithmetic and copies ran while one was open for 1% -> 0% of each run, Pallas kernels for 0% -> 0%
where the time goes in v3:
time: 254 us; the launch traced here: 253 us
  waiting for transfers between devices  126 us (50%)
  matrix products  49.8 us (20%)
  other arithmetic  27.6 us (11%)
  local copies, waits for them, and re-layouts  23.3 us (9%)
  between operations  14.3 us (6%)
  starting transfers between devices  12.3 us (5%)
    unnamed x2, waiting for transfers between devices  96 us
    dot_general x1, matrix products, on_device(): jnp.einsum('skqgcd,qkl->gsc' + 'ld', cross, basis, precision=lax.Precisio...  36.7 us
    ppermute x1, waiting for transfers between devices, padded(): before = lax.ppermute(last, axis, up)  25.6 us
    dot_general x1, matrix products, on_device(): jnp.einsum('qpskwc,pskwd->skqcd', left_both, right_both, preferred_elemen...  13.1 us
    concatenate x1, other arithmetic, padded(): value = jnp.concatenate([before, value, after], axis=dim)  7.73 us
    gather x1, local copies, waits for them, and re-layouts, on_device(): second = jnp.take(extended, local[:, 1], axis=0)  7.21 us
    gather x1, local copies, waits for them, and re-layouts, on_device(): first = jnp.take(extended, local[:, 0], axis=0)  7.21 us
  transfers between devices with their start and end apart: 5, of which 3 were waited for; matrix products, arithmetic and copies ran while one was open for 0% of the time, Pallas kernels for 0%

profile of v3, /device:TPU:1, one launch (start us, length us, event | category | flops | bytes accessed | tf_op | source)
XLA Modules:
  0.0 253.3 jit_solution(3738951187448457212)
XLA Ops:
  6.5 3.7 %copy.30 = bf16[48,2,128,128]{2,0,3,1:T(8,128)(2,1)S(1)} copy(bf16[48,2,128,128]{3,2,1,0:T(8,128)(2,1)} %param.6) | data formatting | bytes 6291456 | tf_op args[0]
  10.2 0.5 convert_element_type.28
  10.7 2.0 fusion.12
  12.8 2.0 reduce
  14.8 0.1 fusion.14
  14.9 0.2 broadcast_in_dim.11
  15.1 1.8 copy.32
  17.0 2.5 fusion.11
  19.4 4.9 %collective-permute-start = (bf16[2,128,48,128]{3,2,1,0:T(8,128)(2,1)}, bf16[2,128,48,128]{3,2,1,0:T(8,128)(2,1)S(1)}, u32[]{:S(2)}, u32[]{:S(2)}) collective-permute-start(bf16[2,128,48,128]{3,2,1,0:T(8,128)(2,1)} %fusion.11), channel_id=1, source_target_pairs={{0,1},{1,2},{2,3},{3,4},{4,5},{5,6},{6,7},{8,9},{9,10},{10,11},{11... | collective-permute-start | bytes 9437192 | tf_op jit(solution)/shard_map/ppermute | solution.py:23
  24.3 1.9 collective-permute-start.1
  26.3 0.1 fusion.21
  26.4 1.3 collective-permute-start.3
  27.6 4.2 %collective-permute-start.2 = (s32[16]{0:T(128)S(1)}, s32[16]{0:T(128)S(1)}, u32[]{:S(2)}, u32[]{:S(2)}) collective-permute-start(s32[16]{0:T(128)S(1)} %get-tuple-element.20), channel_id=1, source_target_pairs={{0,8},{8,16},{16,24},{24,32},{32,40},{40,48},{48,56},{56,64},{64,7... | collective-permute-start | bytes 200 | tf_op jit(solution)/shard_map/ppermute | solution.py:58
  32.6 0.2 fusion.19
  32.8 0.1 maximum_multiply_fusion.1
  32.9 0.1 mul.75
  33.0 0.1 pad_add_fusion
  33.1 0.2 convert_reduce_fusion
  33.3 25.6 %collective-permute-done = bf16[2,128,48,128]{3,2,1,0:T(8,128)(2,1)S(1)} collective-permute-done((bf16[2,128,48,128]{3,2,1,0:T(8,128)(2,1)}, bf16[2,128,48,128]{3,2,1,0:T(8,128)(2,1)S(1)}, u32[]{:S(2)}, u32[]{:S(2)}) %collective-permute-start) | collective-permute-done | bytes 3145760 | tf_op jit(solution)/shard_map/ppermute | solution.py:23
  58.8 4.4 %collective-permute-done.1 = bf16[2,128,48,128]{3,2,1,0:T(8,128)(2,1)} collective-permute-done((bf16[2,128,48,128]{3,2,1,0:T(8,128)(2,1)}, bf16[2,128,48,128]{3,2,1,0:T(8,128)(2,1)}, u32[]{:S(2)}, u32[]{:S(2)}) %collective-permute-start.1) | collective-permute-done | bytes 3145760 | tf_op jit(solution)/shard_map/ppermute | solution.py:24
  63.2 7.7 %pad_maximum_fusion = bf16[6,128,48,128]{3,2,1,0:T(8,128)(2,1)} fusion(bf16[2,128,48,128]{3,2,1,0:T(8,128)(2,1)} %collective-permute-done.1, bf16[2,128,48,128]{3,2,1,0:T(8,128)(2,1)} %fusion.11, bf16[2,128,48,128]{3,2,1,0:T(8,128)(2,1)S(1)} %collective-permute-done), kind=kLoop, calls=%fused_computation.7 | loop fusion | flops 9437184 | bytes 18874368 | tf_op jit(solution)/shard_map/concatenate | solution.py:25
  71.0 7.2 %gather_fusion = bf16[3,128,48,128]{3,2,1,0:T(8,128)(2,1)} fusion(bf16[6,128,48,128]{3,2,1,0:T(8,128)(2,1)} %pad_maximum_fusion, s32[1024]{0:T(1024)S(1)} %get-tuple-element.23), kind=kCustom, calls=%fused_computation.clone | custom fusion | bytes 9437196 | tf_op jit(solution)/shard_map/jit(_take)/gather | solution.py:77
  78.2 3.6 %multiply_convert_fusion = bf16[3,128,48,128]{3,2,1,0:T(8,128)(2,1)S(1)} fusion(bf16[3,128,48,128]{3,2,1,0:T(8,128)(2,1)} %gather_fusion, f32[48]{0:T(128)S(1)} %broadcast_divide_fusion, pred[3]{0:T(512)(128)(4,1)S(1)} %get-tuple-element.18), kind=kLoop, calls=%fused_computation.11 | loop fusion | flops 9437184 | bytes 9437379 | tf_op jit(solution)/shard_map/convert_element_type | solution.py:79
  81.8 3.1 %slice_bitcast_fusion.4 = (bf16[1,3,64,48,128]{4,3,2,1,0:T(8,128)(2,1)}, bf16[1,3,64,48,128]{4,3,0,2,1:T(8,128)(2,1)S(1)}, bf16[1,3,64,48,128]{4,3,0,2,1:T(8,128)(2,1)}, bf16[1,3,64,48,128]{4,3,2,1,0:T(8,128)(2,1)}) fusion(bf16[3,128,48,128]{3,2,1,0:T(8,128)(2,1)S(1)} %multiply_convert_fusion), kind=kLoop, calls=%fused_computation.29 | loop fusion | flops 1179648 | bytes 14155776 | tf_op jit(solution)/shard_map/stack | solution.py:82
  84.9 7.2 %gather_fusion.1 = bf16[3,128,48,128]{3,2,1,0:T(8,128)(2,1)} fusion(bf16[6,128,48,128]{3,2,1,0:T(8,128)(2,1)} %pad_maximum_fusion, s32[1024]{0:T(1024)S(1)} %get-tuple-element.22), kind=kCustom, calls=%fused_computation.1.clone | custom fusion | bytes 9437196 | tf_op jit(solution)/shard_map/jit(_take)/gather | solution.py:78
  92.2 2.9 %broadcast_select_fusion = bf16[3,128,48,128]{3,2,1,0:T(8,128)(2,1)S(1)} fusion(bf16[3,128,48,128]{3,2,1,0:T(8,128)(2,1)} %gather_fusion.1, pred[3]{0:T(512)(128)(4,1)S(1)} %get-tuple-element.6), kind=kLoop, calls=%fused_computation.19 | loop fusion | flops 2359296 | bytes 9437187 | tf_op jit(solution)/shard_map/jit(_take)/select_n | solution.py:78
  95.0 3.0 %slice_bitcast_fusion.1 = (bf16[1,3,64,48,128]{4,3,0,2,1:T(8,128)(2,1)}, bf16[1,3,64,48,128]{4,3,0,2,1:T(8,128)(2,1)}) fusion(bf16[3,128,48,128]{3,2,1,0:T(8,128)(2,1)S(1)} %broadcast_select_fusion), kind=kLoop, calls=%fused_computation.25 | loop fusion | bytes 9437184 | tf_op jit(solution)/shard_map/stack | solution.py:83
  98.0 2.6 %maximum_bitcast_fusion.1 = bf16[1,2,3,64,48,128]{5,4,1,0,3,2:T(8,128)(2,1)} fusion(bf16[1,3,64,48,128]{4,3,0,2,1:T(8,128)(2,1)S(1)} %get-tuple-element.13, bf16[1,3,64,48,128]{4,3,0,2,1:T(8,128)(2,1)S(1)} %copy-done), kind=kLoop, calls=%fused_computation.15 | loop fusion | flops 2359296 | bytes 9437184 | tf_op jit(solution)/shard_map/stack | solution.py:82
  100.6 13.1 %convolution_bitcast_fusion = f32[3,64,2,16,8,128]{5,4,3,2,1,0:T(8,128)} fusion(bf16[1,2,3,64,48,128]{5,4,1,0,3,2:T(8,128)(2,1)} %maximum_bitcast_fusion.1, bf16[1,3,64,48,128]{4,3,0,2,1:T(8,128)(2,1)} %get-tuple-element.11, bf16[1,3,64,48,128]{4,3,0,2,1:T(8,128)(2,1)} %get-tuple-element.10, bf16[1,3,64,48,128]{4,3,2,1,0:T(8,128)(2,1)} %get-tuple-element.15, ...), kind=kOutput, calls=%fused_computation.6 | convolution fusion | flops 1231552512 | bytes 39321600 | tf_op jit(solution)/shard_map/qpskwc,pskwd->skqcd/dot_general | solution.py:84
  113.7 36.7 %fusion.2 = f32[16,3,8,64,128]{4,3,2,1,0:T(8,128)} fusion(f32[3]{0:T(128)S(1)} %compare_convert_fusion, f32[3,64,2,16,8,128]{5,4,3,2,1,0:T(8,128)} %convolution_bitcast_fusion, f32[2,64,64,1,1,1]{1,0,2,5,4,3:T(2,128)S(1)} %bitcast.59), kind=kOutput, calls=%fused_computation.5 | convolution fusion | flops 4834983936 | bytes 37781516 | tf_op jit(solution)/shard_map/skqgcd,qkl->gscld/dot_general | solution.py:90
  150.4 0.0 reduce-scatter.4.cloned.1.call-update
  150.4 96.0 %reduce-scatter.4.cloned.1.call-done = f32[1,3,8,64,128]{4,3,2,1,0:T(8,128)} async-done(((f32[16,3,8,64,128]{4,3,2,1,0:T(8,128)}), f32[1,3,8,64,128]{4,3,2,1,0:T(8,128)}) %reduce-scatter.4.cloned.1.call-update) | async-done | bytes 786448
  (18 shorter events, 0.1 us)
Async XLA Ops:
  6.5 239.9 %reduce-scatter.4.cloned.1.call-start = ((), (), s32[]{:S(2)}) async-start(), calls=%async_computation.1 | async-start | bytes 13369344
  16.9 9.3 %copy-start.2 = (s32[48]{0:T(128)S(1)}, s32[48]{0:T(128)}, u32[]{:S(2)}) copy-start(s32[48]{0:T(128)} %param.7) | copy-start | bytes 580
  16.9 15.6 %copy-start.1 = (s32[3,2]{0,1:T(2,128)S(1)}, s32[3,2]{0,1:T(2,128)}, u32[]{:S(2)}) copy-start(s32[3,2]{0,1:T(2,128)} %param.8) | copy-start | bytes 76
  19.4 39.4 %collective-permute-start = (bf16[2,128,48,128]{3,2,1,0:T(8,128)(2,1)}, bf16[2,128,48,128]{3,2,1,0:T(8,128)(2,1)S(1)}, u32[]{:S(2)}, u32[]{:S(2)}) collective-permute-start(bf16[2,128,48,128]{3,2,1,0:T(8,128)(2,1)} %fusion.11), channel_id=1, source_target_pairs={{0,1},{1,2},{2,3},{3,4},{4,5},{5,6},{6,7},{8,9},{9,10},{10,11},{11... | collective-permute-start | bytes 9437192 | tf_op jit(solution)/shard_map/ppermute | solution.py:23
  24.3 38.9 %collective-permute-start.1 = (bf16[2,128,48,128]{3,2,1,0:T(8,128)(2,1)}, bf16[2,128,48,128]{3,2,1,0:T(8,128)(2,1)}, u32[]{:S(2)}, u32[]{:S(2)}) collective-permute-start(bf16[2,128,48,128]{3,2,1,0:T(8,128)(2,1)} %fusion.11), channel_id=1, source_target_pairs={{1,0},{2,1},{3,2},{4,3},{5,4},{6,5},{7,6},{9,8},{10,9},{11,10},{12... | collective-permute-start | bytes 9437192 | tf_op jit(solution)/shard_map/ppermute | solution.py:24
  26.4 6.6 %collective-permute-start.3 = (s32[16]{0:T(128)S(1)}, s32[16]{0:T(128)S(1)}, u32[]{:S(2)}, u32[]{:S(2)}) collective-permute-start(s32[16]{0:T(128)S(1)} %get-tuple-element.21), channel_id=1, source_target_pairs={{8,0},{16,8},{24,16},{32,24},{40,32},{48,40},{56,48},{64,56},{72,6... | collective-permute-start | bytes 200 | tf_op jit(solution)/shard_map/ppermute | solution.py:59
  27.6 5.3 %collective-permute-start.2 = (s32[16]{0:T(128)S(1)}, s32[16]{0:T(128)S(1)}, u32[]{:S(2)}, u32[]{:S(2)}) collective-permute-start(s32[16]{0:T(128)S(1)} %get-tuple-element.20), channel_id=1, source_target_pairs={{0,8},{8,16},{16,24},{24,32},{32,40},{40,48},{48,56},{56,64},{64,7... | collective-permute-start | bytes 200 | tf_op jit(solution)/shard_map/ppermute | solution.py:58
  95.0 3.0 %copy-start = (bf16[1,3,64,48,128]{4,3,0,2,1:T(8,128)(2,1)S(1)}, bf16[1,3,64,48,128]{4,3,0,2,1:T(8,128)(2,1)}, u32[]{:S(2)}) copy-start(bf16[1,3,64,48,128]{4,3,0,2,1:T(8,128)(2,1)} %get-tuple-element.14) | copy-start | bytes 7077892
Sparse Core Ops, SparseCore 0:
  150.6 95.8 reduce-scatter.3

commit v4 on v3

--- a/solution.py
+++ b/solution.py
@@ -88,7 +88,7 @@
     channels = cross.shape[3]
     cross = cross.reshape(slot_total, FB, 2, win_count, channels // win_count, channels)
     corr = jnp.einsum(
-        "skqgcd,qkl->gsc" + "ld", cross, basis, precision=lax.Precision.HIGHEST
+        "skqgcd,qkl->gscld", cross, basis, precision=lax.Precision.HIGH
     )
     corr = corr * live[None, :, None, None, None]
     corr = with_layout_constraint(corr, Layout((0, 1, 2, 3, 4)))

time: 254 us -> 250 us (0.984)
  matrix products: 49.8 us -> 46 us
    dot_general x1, matrix products: 36.7 us -> 32.9 us  [on_device(): jnp.einsum('skqgcd,qkl->gscld', cross, basis, precision=lax.Precision.HIGH)]
where the time goes in v4:
time: 250 us; the launch traced here: 249 us
  waiting for transfers between devices  126 us (50%)
  matrix products  46 us (18%)
  other arithmetic  27.6 us (11%)
  local copies, waits for them, and re-layouts  23.3 us (9%)
  between operations  14.3 us (6%)
  starting transfers between devices  12.3 us (5%)
    unnamed x2, waiting for transfers between devices  96 us
    dot_general x1, matrix products, on_device(): jnp.einsum('skqgcd,qkl->gscld', cross, basis, precision=lax.Precision.HIGH)  32.9 us
    ppermute x1, waiting for transfers between devices, padded(): before = lax.ppermute(last, axis, up)  25.6 us
    dot_general x1, matrix products, on_device(): jnp.einsum('qpskwc,pskwd->skqcd', left_both, right_both, preferred_elemen...  13.1 us
    concatenate x1, other arithmetic, padded(): value = jnp.concatenate([before, value, after], axis=dim)  7.73 us
    gather x1, local copies, waits for them, and re-layouts, on_device(): second = jnp.take(extended, local[:, 1], axis=0)  7.21 us
    gather x1, local copies, waits for them, and re-layouts, on_device(): first = jnp.take(extended, local[:, 0], axis=0)  7.21 us
  transfers between devices with their start and end apart: 5, of which 3 were waited for; matrix products, arithmetic and copies ran while one was open for 0% of the time, Pallas kernels for 0%

profile of v4, /device:TPU:1, one launch (start us, length us, event | category | flops | bytes accessed | tf_op | source)
XLA Modules:
  0.0 249.4 jit_solution(10580948685227593932)
XLA Ops:
  6.5 3.7 %copy.30 = bf16[48,2,128,128]{2,0,3,1:T(8,128)(2,1)S(1)} copy(bf16[48,2,128,128]{3,2,1,0:T(8,128)(2,1)} %param.6) | data formatting | bytes 6291456 | tf_op args[0]
  10.2 0.5 convert_element_type.28
  10.7 2.0 fusion.12
  12.8 2.0 reduce
  14.8 0.1 fusion.14
  14.9 0.2 broadcast_in_dim.11
  15.1 1.8 copy.32
  17.0 2.5 fusion.11
  19.4 4.9 %collective-permute-start = (bf16[2,128,48,128]{3,2,1,0:T(8,128)(2,1)}, bf16[2,128,48,128]{3,2,1,0:T(8,128)(2,1)S(1)}, u32[]{:S(2)}, u32[]{:S(2)}) collective-permute-start(bf16[2,128,48,128]{3,2,1,0:T(8,128)(2,1)} %fusion.11), channel_id=1, source_target_pairs={{0,1},{1,2},{2,3},{3,4},{4,5},{5,6},{6,7},{8,9},{9,10},{10,11},{11... | collective-permute-start | bytes 9437192 | tf_op jit(solution)/shard_map/ppermute | solution.py:23
  24.3 1.9 collective-permute-start.1
  26.3 0.1 fusion.21
  26.4 1.3 collective-permute-start.3
  27.6 4.2 %collective-permute-start.2 = (s32[16]{0:T(128)S(1)}, s32[16]{0:T(128)S(1)}, u32[]{:S(2)}, u32[]{:S(2)}) collective-permute-start(s32[16]{0:T(128)S(1)} %get-tuple-element.20), channel_id=1, source_target_pairs={{0,8},{8,16},{16,24},{24,32},{32,40},{40,48},{48,56},{56,64},{64,7... | collective-permute-start | bytes 200 | tf_op jit(solution)/shard_map/ppermute | solution.py:58
  32.6 0.2 fusion.19
  32.8 0.1 maximum_multiply_fusion.1
  32.9 0.1 mul.75
  33.0 0.1 pad_add_fusion
  33.1 0.2 convert_reduce_fusion
  33.3 25.6 %collective-permute-done = bf16[2,128,48,128]{3,2,1,0:T(8,128)(2,1)S(1)} collective-permute-done((bf16[2,128,48,128]{3,2,1,0:T(8,128)(2,1)}, bf16[2,128,48,128]{3,2,1,0:T(8,128)(2,1)S(1)}, u32[]{:S(2)}, u32[]{:S(2)}) %collective-permute-start) | collective-permute-done | bytes 3145760 | tf_op jit(solution)/shard_map/ppermute | solution.py:23
  58.8 4.4 %collective-permute-done.1 = bf16[2,128,48,128]{3,2,1,0:T(8,128)(2,1)} collective-permute-done((bf16[2,128,48,128]{3,2,1,0:T(8,128)(2,1)}, bf16[2,128,48,128]{3,2,1,0:T(8,128)(2,1)}, u32[]{:S(2)}, u32[]{:S(2)}) %collective-permute-start.1) | collective-permute-done | bytes 3145760 | tf_op jit(solution)/shard_map/ppermute | solution.py:24
  63.2 7.7 %pad_maximum_fusion = bf16[6,128,48,128]{3,2,1,0:T(8,128)(2,1)} fusion(bf16[2,128,48,128]{3,2,1,0:T(8,128)(2,1)} %collective-permute-done.1, bf16[2,128,48,128]{3,2,1,0:T(8,128)(2,1)} %fusion.11, bf16[2,128,48,128]{3,2,1,0:T(8,128)(2,1)S(1)} %collective-permute-done), kind=kLoop, calls=%fused_computation.7 | loop fusion | flops 9437184 | bytes 18874368 | tf_op jit(solution)/shard_map/concatenate | solution.py:25
  71.0 7.2 %gather_fusion = bf16[3,128,48,128]{3,2,1,0:T(8,128)(2,1)} fusion(bf16[6,128,48,128]{3,2,1,0:T(8,128)(2,1)} %pad_maximum_fusion, s32[1024]{0:T(1024)S(1)} %get-tuple-element.23), kind=kCustom, calls=%fused_computation.clone | custom fusion | bytes 9437196 | tf_op jit(solution)/shard_map/jit(_take)/gather | solution.py:77
  78.2 3.6 %multiply_convert_fusion = bf16[3,128,48,128]{3,2,1,0:T(8,128)(2,1)S(1)} fusion(bf16[3,128,48,128]{3,2,1,0:T(8,128)(2,1)} %gather_fusion, f32[48]{0:T(128)S(1)} %broadcast_divide_fusion, pred[3]{0:T(512)(128)(4,1)S(1)} %get-tuple-element.18), kind=kLoop, calls=%fused_computation.11 | loop fusion | flops 9437184 | bytes 9437379 | tf_op jit(solution)/shard_map/convert_element_type | solution.py:79
  81.8 3.1 %slice_bitcast_fusion.4 = (bf16[1,3,64,48,128]{4,3,2,1,0:T(8,128)(2,1)}, bf16[1,3,64,48,128]{4,3,0,2,1:T(8,128)(2,1)S(1)}, bf16[1,3,64,48,128]{4,3,0,2,1:T(8,128)(2,1)}, bf16[1,3,64,48,128]{4,3,2,1,0:T(8,128)(2,1)}) fusion(bf16[3,128,48,128]{3,2,1,0:T(8,128)(2,1)S(1)} %multiply_convert_fusion), kind=kLoop, calls=%fused_computation.29 | loop fusion | flops 1179648 | bytes 14155776 | tf_op jit(solution)/shard_map/stack | solution.py:82
  84.9 7.2 %gather_fusion.1 = bf16[3,128,48,128]{3,2,1,0:T(8,128)(2,1)} fusion(bf16[6,128,48,128]{3,2,1,0:T(8,128)(2,1)} %pad_maximum_fusion, s32[1024]{0:T(1024)S(1)} %get-tuple-element.22), kind=kCustom, calls=%fused_computation.1.clone | custom fusion | bytes 9437196 | tf_op jit(solution)/shard_map/jit(_take)/gather | solution.py:78
  92.2 2.9 %broadcast_select_fusion = bf16[3,128,48,128]{3,2,1,0:T(8,128)(2,1)S(1)} fusion(bf16[3,128,48,128]{3,2,1,0:T(8,128)(2,1)} %gather_fusion.1, pred[3]{0:T(512)(128)(4,1)S(1)} %get-tuple-element.6), kind=kLoop, calls=%fused_computation.19 | loop fusion | flops 2359296 | bytes 9437187 | tf_op jit(solution)/shard_map/jit(_take)/select_n | solution.py:78
  95.0 3.0 %slice_bitcast_fusion.1 = (bf16[1,3,64,48,128]{4,3,0,2,1:T(8,128)(2,1)}, bf16[1,3,64,48,128]{4,3,0,2,1:T(8,128)(2,1)}) fusion(bf16[3,128,48,128]{3,2,1,0:T(8,128)(2,1)S(1)} %broadcast_select_fusion), kind=kLoop, calls=%fused_computation.25 | loop fusion | bytes 9437184 | tf_op jit(solution)/shard_map/stack | solution.py:83
  98.0 2.6 %maximum_bitcast_fusion.1 = bf16[1,2,3,64,48,128]{5,4,1,0,3,2:T(8,128)(2,1)} fusion(bf16[1,3,64,48,128]{4,3,0,2,1:T(8,128)(2,1)S(1)} %get-tuple-element.13, bf16[1,3,64,48,128]{4,3,0,2,1:T(8,128)(2,1)S(1)} %copy-done), kind=kLoop, calls=%fused_computation.15 | loop fusion | flops 2359296 | bytes 9437184 | tf_op jit(solution)/shard_map/stack | solution.py:82
  100.6 13.1 %convolution_bitcast_fusion = f32[3,64,2,16,8,128]{5,4,3,2,1,0:T(8,128)} fusion(bf16[1,2,3,64,48,128]{5,4,1,0,3,2:T(8,128)(2,1)} %maximum_bitcast_fusion.1, bf16[1,3,64,48,128]{4,3,0,2,1:T(8,128)(2,1)} %get-tuple-element.11, bf16[1,3,64,48,128]{4,3,0,2,1:T(8,128)(2,1)} %get-tuple-element.10, bf16[1,3,64,48,128]{4,3,2,1,0:T(8,128)(2,1)} %get-tuple-element.15, ...), kind=kOutput, calls=%fused_computation.6 | convolution fusion | flops 1231552512 | bytes 39321600 | tf_op jit(solution)/shard_map/qpskwc,pskwd->skqcd/dot_general | solution.py:84
  113.7 32.9 %fusion.2 = f32[16,3,8,64,128]{4,3,2,1,0:T(8,128)} fusion(f32[3]{0:T(128)S(1)} %compare_convert_fusion, f32[3,64,2,16,8,128]{5,4,3,2,1,0:T(8,128)} %convolution_bitcast_fusion, f32[2,64,64,1,1,1]{1,0,2,5,4,3:T(2,128)S(1)} %bitcast.59), kind=kOutput, calls=%fused_computation.5 | convolution fusion | flops 2419064832 | bytes 37781516 | tf_op jit(solution)/shard_map/skqgcd,qkl->gscld/dot_general | solution.py:90
  146.6 0.0 reduce-scatter.4.cloned.1.call-update
  146.6 95.9 %reduce-scatter.4.cloned.1.call-done = f32[1,3,8,64,128]{4,3,2,1,0:T(8,128)} async-done(((f32[16,3,8,64,128]{4,3,2,1,0:T(8,128)}), f32[1,3,8,64,128]{4,3,2,1,0:T(8,128)}) %reduce-scatter.4.cloned.1.call-update) | async-done | bytes 786448
  (18 shorter events, 0.1 us)
Async XLA Ops:
  6.5 236.0 %reduce-scatter.4.cloned.1.call-start = ((), (), s32[]{:S(2)}) async-start(), calls=%async_computation.1 | async-start | bytes 13369344
  16.9 9.3 %copy-start.2 = (s32[48]{0:T(128)S(1)}, s32[48]{0:T(128)}, u32[]{:S(2)}) copy-start(s32[48]{0:T(128)} %param.7) | copy-start | bytes 580
  16.9 15.6 %copy-start.1 = (s32[3,2]{0,1:T(2,128)S(1)}, s32[3,2]{0,1:T(2,128)}, u32[]{:S(2)}) copy-start(s32[3,2]{0,1:T(2,128)} %param.8) | copy-start | bytes 76
  19.4 39.4 %collective-permute-start = (bf16[2,128,48,128]{3,2,1,0:T(8,128)(2,1)}, bf16[2,128,48,128]{3,2,1,0:T(8,128)(2,1)S(1)}, u32[]{:S(2)}, u32[]{:S(2)}) collective-permute-start(bf16[2,128,48,128]{3,2,1,0:T(8,128)(2,1)} %fusion.11), channel_id=1, source_target_pairs={{0,1},{1,2},{2,3},{3,4},{4,5},{5,6},{6,7},{8,9},{9,10},{10,11},{11... | collective-permute-start | bytes 9437192 | tf_op jit(solution)/shard_map/ppermute | solution.py:23
  24.3 38.9 %collective-permute-start.1 = (bf16[2,128,48,128]{3,2,1,0:T(8,128)(2,1)}, bf16[2,128,48,128]{3,2,1,0:T(8,128)(2,1)}, u32[]{:S(2)}, u32[]{:S(2)}) collective-permute-start(bf16[2,128,48,128]{3,2,1,0:T(8,128)(2,1)} %fusion.11), channel_id=1, source_target_pairs={{1,0},{2,1},{3,2},{4,3},{5,4},{6,5},{7,6},{9,8},{10,9},{11,10},{12... | collective-permute-start | bytes 9437192 | tf_op jit(solution)/shard_map/ppermute | solution.py:24
  26.4 6.6 %collective-permute-start.3 = (s32[16]{0:T(128)S(1)}, s32[16]{0:T(128)S(1)}, u32[]{:S(2)}, u32[]{:S(2)}) collective-permute-start(s32[16]{0:T(128)S(1)} %get-tuple-element.21), channel_id=1, source_target_pairs={{8,0},{16,8},{24,16},{32,24},{40,32},{48,40},{56,48},{64,56},{72,6... | collective-permute-start | bytes 200 | tf_op jit(solution)/shard_map/ppermute | solution.py:59
  27.6 5.3 %collective-permute-start.2 = (s32[16]{0:T(128)S(1)}, s32[16]{0:T(128)S(1)}, u32[]{:S(2)}, u32[]{:S(2)}) collective-permute-start(s32[16]{0:T(128)S(1)} %get-tuple-element.20), channel_id=1, source_target_pairs={{0,8},{8,16},{16,24},{24,32},{32,40},{40,48},{48,56},{56,64},{64,7... | collective-permute-start | bytes 200 | tf_op jit(solution)/shard_map/ppermute | solution.py:58
  95.0 3.0 %copy-start = (bf16[1,3,64,48,128]{4,3,0,2,1:T(8,128)(2,1)S(1)}, bf16[1,3,64,48,128]{4,3,0,2,1:T(8,128)(2,1)}, u32[]{:S(2)}) copy-start(bf16[1,3,64,48,128]{4,3,0,2,1:T(8,128)(2,1)} %get-tuple-element.14) | copy-start | bytes 7077892
Sparse Core Ops, SparseCore 0:
  146.7 95.7 reduce-scatter.3

commit v5 on v4

--- a/solution.py
+++ b/solution.py
@@ -74,8 +74,12 @@
     live_count = pair_count[0]
     win_count = lax.axis_size("win")
     local = jnp.clip(pair_blocks - first_local, 0, extended.shape[0] - 1)
-    first = jnp.take(extended, local[:, 0], axis=0)
-    second = jnp.take(extended, local[:, 1], axis=0)
+    first = jnp.stack(
+        [lax.dynamic_index_in_dim(extended, local[i, 0], 0, False) for i in range(slot_total)]
+    )
+    second = jnp.stack(
+        [lax.dynamic_index_in_dim(extended, local[i, 1], 0, False) for i in range(slot_total)]
+    )
     left = (first.astype(jnp.float32) * weight[None, None, :, None]).astype(jnp.bfloat16)
     left_real, left_imag = (left[:, :FB], left[:, FB:])
     right_real, right_imag = (second[:, :FB], second[:, FB:])

time: 250 us -> 227 us (0.908)
  local copies, waits for them, and re-layouts: 23.3 us -> 10.9 us
  waiting for transfers between devices: 126 us -> 114 us
  between operations: 14.3 us -> 25.8 us
  other arithmetic: 27.6 us -> 18.8 us
    gather x2 -> x0, local copies, waits for them, and re-layouts: 14.4 us -> none  [the longest x1 7.21 us: on_device(): second = jnp.take(extended, local[:, 1], axis=0)]
    ppermute x1, waiting for transfers between devices: 25.6 us -> 13.6 us  [padded(): before = lax.ppermute(last, axis, up)]
    dynamic_slice x0 -> x1, local copies, waits for them, and re-layouts: none -> 3.28 us  [on_device(): lax.dynamic_index_in_dim(extended, local[i, 1], 0, False)]
    concatenate x1, other arithmetic: 7.73 us -> 4.64 us  [padded(): value = jnp.concatenate([before, value, after], axis=dim)]
    select_n x1 -> x0, other arithmetic: 2.85 us -> none  [on_device(): second = jnp.take(extended, local[:, 1], axis=0)]
    another operation x1, other arithmetic: 3.13 us -> 0.61 us  [on_device(): jnp.stack([left_real, left_imag])]
  transfers between devices with their start and end apart: 5 -> 5, of which waited for: 3 -> 3; matrix products, arithmetic and copies ran while one was open for 0% -> 1% of each run, Pallas kernels for 0% -> 0%
where the time goes in v5:
time: 227 us
  waiting for transfers between devices  114 us (50%)
  matrix products  45.3 us (20%)
  between operations  25.8 us (11%)
  other arithmetic  18.8 us (8%)
  starting transfers between devices  12.1 us (5%)
  local copies, waits for them, and re-layouts  10.9 us (5%)
    unnamed x2, waiting for transfers between devices  95.9 us
    dot_general x1, matrix products, on_device(): jnp.einsum('skqgcd,qkl->gscld', cross, basis, precision=lax.Precision.HIGH)  32.9 us
    ppermute x1, waiting for transfers between devices, padded(): before = lax.ppermute(last, axis, up)  13.6 us
    dot_general x1, matrix products, on_device(): jnp.einsum('qpskwc,pskwd->skqcd', left_both, right_both, preferred_elemen...  12.5 us
    ppermute x1, starting transfers between devices, padded(): before = lax.ppermute(last, axis, up)  4.91 us
    concatenate x1, other arithmetic, padded(): value = jnp.concatenate([before, value, after], axis=dim)  4.64 us
  transfers between devices with their start and end apart: 5, of which 3 were waited for; matrix products, arithmetic and copies ran while one was open for 1% of the time, Pallas kernels for 0%

profile of v5, /device:TPU:1, one launch (start us, length us, event | category | flops | bytes accessed | tf_op | source)
XLA Modules:
  0.0 226.9 jit_solution(3110668715224557975)
XLA Ops:
  6.5 3.7 %copy.22 = bf16[48,2,128,128]{2,0,3,1:T(8,128)(2,1)S(1)} copy(bf16[48,2,128,128]{3,2,1,0:T(8,128)(2,1)} %param.4) | data formatting | bytes 6291456 | tf_op args[0]
  10.2 0.5 convert_element_type.28
  10.7 2.0 fusion.10
  12.8 2.0 reduce_sum.18
  14.8 0.2 broadcast_in_dim.2
  15.1 0.0 copy-start.1
  15.1 0.0 copy-start
  15.1 2.5 %fusion.9 = bf16[2,128,48,128]{3,2,1,0:T(8,128)(2,1)} fusion(f32[48,2,128,64]{2,0,3,1:T(8,128)S(1)} %bitcast.49, bf16[48,2,128,128]{2,0,3,1:T(8,128)(2,1)S(1)} %copy.22), kind=kLoop, calls=%fused_computation.17 | loop fusion | flops 6291456 | bytes 9437184 | tf_op jit(solution)/shard_map/transpose | solution.py:40
  17.5 4.9 %collective-permute-start = (bf16[2,128,48,128]{3,2,1,0:T(8,128)(2,1)}, bf16[2,128,48,128]{3,2,1,0:T(8,128)(2,1)S(1)}, u32[]{:S(2)}, u32[]{:S(2)}) collective-permute-start(bf16[2,128,48,128]{3,2,1,0:T(8,128)(2,1)} %fusion.9), channel_id=1, source_target_pairs={{0,1},{1,2},{2,3},{3,4},{4,5},{5,6},{6,7},{8,9},{9,10},{10,11},{11... | collective-permute-start | bytes 9437192 | tf_op jit(solution)/shard_map/ppermute | solution.py:23
  22.5 1.9 collective-permute-start.1
  24.4 0.1 fusion.18
  24.5 1.3 collective-permute-start.3
  25.8 4.0 %collective-permute-start.2 = (s32[16]{0:T(128)S(1)}, s32[16]{0:T(128)S(1)}, u32[]{:S(2)}, u32[]{:S(2)}) collective-permute-start(s32[16]{0:T(128)S(1)} %get-tuple-element.26), channel_id=1, source_target_pairs={{0,8},{8,16},{16,24},{24,32},{32,40},{40,48},{48,56},{56,64},{64,7... | collective-permute-start | bytes 200 | tf_op jit(solution)/shard_map/ppermute | solution.py:58
  29.8 0.7 fusion.17
  38.2 0.2 fusion.15
  38.4 0.1 maximum_multiply_fusion.1
  38.5 0.1 mul.75
  43.1 0.1 pad_add_fusion
  43.2 0.2 convert_reduce_fusion
  43.4 13.6 %collective-permute-done = bf16[2,128,48,128]{3,2,1,0:T(8,128)(2,1)S(1)} collective-permute-done((bf16[2,128,48,128]{3,2,1,0:T(8,128)(2,1)}, bf16[2,128,48,128]{3,2,1,0:T(8,128)(2,1)S(1)}, u32[]{:S(2)}, u32[]{:S(2)}) %collective-permute-start) | collective-permute-done | bytes 3145760 | tf_op jit(solution)/shard_map/ppermute | solution.py:23
  57.0 4.4 %collective-permute-done.1 = bf16[2,128,48,128]{3,2,1,0:T(8,128)(2,1)} collective-permute-done((bf16[2,128,48,128]{3,2,1,0:T(8,128)(2,1)}, bf16[2,128,48,128]{3,2,1,0:T(8,128)(2,1)}, u32[]{:S(2)}, u32[]{:S(2)}) %collective-permute-start.1) | collective-permute-done | bytes 3145760 | tf_op jit(solution)/shard_map/ppermute | solution.py:24
  61.4 4.6 %pad_maximum_fusion = bf16[6,128,48,128]{3,2,1,0:T(8,128)(2,1)S(1)} fusion(bf16[2,128,48,128]{3,2,1,0:T(8,128)(2,1)} %collective-permute-done.1, bf16[2,128,48,128]{3,2,1,0:T(8,128)(2,1)} %fusion.9, bf16[2,128,48,128]{3,2,1,0:T(8,128)(2,1)S(1)} %collective-permute-done), kind=kLoop, calls=%fused_computation.5 | loop fusion | flops 9437184 | bytes 18874368 | tf_op jit(solution)/shard_map/concatenate | solution.py:25
  66.0 3.3 %constant_dynamic-slice_fusion.2 = (bf16[1,128,48,128]{3,2,1,0:T(8,128)(2,1)S(1)}, bf16[1,128,48,128]{3,2,1,0:T(8,128)(2,1)S(1)}, bf16[1,128,48,128]{3,2,1,0:T(8...) fusion(bf16[6,128,48,128]{3,2,1,0:T(8,128)(2,1)S(1)} %pad_maxim, ...), kind=kLoop, calls=%fused_computation.43 | loop fusion | bytes 18874392 | tf_op jit(solution)/shard_map/jit(dynamic_index_in_dim)/dynamic_slice | solution.py:81
  69.3 2.5 %multiply_convert_fusion = bf16[3,128,48,128]{3,2,1,0:T(8,128)(2,1)S(1)} fusion(bf16[1,128,48,128]{3,2,1,0:T(8,128)(2,1)S(1)} %get-tuple-element.8, bf16[1,128,48,128]{3,2,1,0:T(8,128)(2,1)} %get-tuple-element.9, bf16[1,128,48,128]{3,2,1,0:T(8,128)(2,1)} %get-tuple-element.10, f32[48]{0:T(128)S(1)} %broadcast_divide_fusion), kind=kLoop, calls=%fused_computation.8 | loop fusion | flops 11796480 | bytes 9437376 | tf_op jit(solution)/shard_map/convert_element_type | solution.py:83
  71.8 0.6 slice_bitcast_fusion.3
  72.4 0.6 pad_maximum_fusion.2
  73.0 2.9 %slice_bitcast_fusion.1 = (bf16[1,3,64,48,128]{4,3,0,2,1:T(8,128)(2,1)}, bf16[1,3,64,48,128]{4,3,0,2,1:T(8,128)(2,1)}) fusion(bf16[3,128,48,128]{3,2,1,0:T(8,128)(2,1)S(1)} %pad_maximum_fusion.2), kind=kLoop, calls=%fused_computation.22 | loop fusion | bytes 9437184 | tf_op jit(solution)/shard_map/stack | solution.py:87
  75.9 2.9 %maximum_bitcast_fusion = (bf16[1,2,3,64,48,128]{5,4,3,2,1,0:T(8,128)(2,1)S(1)}, bf16[1,2,3,64,48,128]{5,4,3,2,1,0:T(8,128)(2,1)}) fusion(bf16[1,3,64,48,128]{4,3,2,1,0:T(8,128)(2,1)S(1)} %get-tuple-element.15, bf16[1,3,64,48,128]{4,3,2,1,0:T(8,128)(2,1)S(1)} %get-tuple-element.13, bf16[1,3,64,48,128]{4,3,2,1,0:T(8,128)(2,1)S(1)} %get-tuple-element.14), kind=kLoop, calls=%fused_computation.11 | loop fusion | flops 4718592 | bytes 16515072 | tf_op jit(solution)/shard_map/stack | solution.py:86
  78.8 12.5 %convolution_bitcast_fusion = f32[3,64,2,16,8,128]{5,4,3,2,1,0:T(8,128)} fusion(bf16[1,3,64,48,128]{4,3,0,2,1:T(8,128)(2,1)} %get-tuple-element.12, bf16[1,3,64,48,128]{4,3,0,2,1:T(8,128)(2,1)} %get-tuple-element.11, bf16[1,2,3,64,48,128]{5,4,3,2,1,0:T(8,128)(2,1)} %get-tuple-element.17, bf16[1,2,3,64,48,128]{5,4,3,2,1,0:T(8,128)(2,1)S(1)} %get-tuple-element.16), kind=kOutput, calls=%fused_computation.4 | convolution fusion | flops 1215037440 | bytes 39321600 | tf_op jit(solution)/shard_map/qpskwc,pskwd->skqcd/dot_general | solution.py:88
  91.2 32.9 %fusion.2 = f32[16,3,8,64,128]{4,3,2,1,0:T(8,128)} fusion(f32[3]{0:T(128)S(1)} %compare_convert_fusion, f32[3,64,2,16,8,128]{5,4,3,2,1,0:T(8,128)} %convolution_bitcast_fusion, f32[2,64,64,1,1,1]{1,0,2,5,4,3:T(2,128)S(1)} %bitcast.51), kind=kOutput, calls=%fused_computation.3 | convolution fusion | flops 2419064832 | bytes 37781516 | tf_op jit(solution)/shard_map/skqgcd,qkl->gscld/dot_general | solution.py:94
  124.1 0.0 reduce-scatter.4.cloned.1.call-update
  124.1 95.9 %reduce-scatter.4.cloned.1.call-done = f32[1,3,8,64,128]{4,3,2,1,0:T(8,128)} async-done(((f32[16,3,8,64,128]{4,3,2,1,0:T(8,128)}), f32[1,3,8,64,128]{4,3,2,1,0:T(8,128)}) %reduce-scatter.4.cloned.1.call-update) | async-done | bytes 786448
  (13 shorter events, 0.1 us)
Async XLA Ops:
  6.5 213.5 %reduce-scatter.4.cloned.1.call-start = ((), (), s32[]{:S(2)}) async-start(), calls=%async_computation.1 | async-start | bytes 13369344
  15.1 9.3 %copy-start.1 = (s32[48]{0:T(128)S(1)}, s32[48]{0:T(128)}, u32[]{:S(2)}) copy-start(s32[48]{0:T(128)} %param.5) | copy-start | bytes 580
  15.1 14.7 %copy-start = (s32[3,2]{0,1:T(2,128)S(1)}, s32[3,2]{0,1:T(2,128)}, u32[]{:S(2)}) copy-start(s32[3,2]{0,1:T(2,128)} %param.6) | copy-start | bytes 76
  17.5 39.4 %collective-permute-start = (bf16[2,128,48,128]{3,2,1,0:T(8,128)(2,1)}, bf16[2,128,48,128]{3,2,1,0:T(8,128)(2,1)S(1)}, u32[]{:S(2)}, u32[]{:S(2)}) collective-permute-start(bf16[2,128,48,128]{3,2,1,0:T(8,128)(2,1)} %fusion.9), channel_id=1, source_target_pairs={{0,1},{1,2},{2,3},{3,4},{4,5},{5,6},{6,7},{8,9},{9,10},{10,11},{11... | collective-permute-start | bytes 9437192 | tf_op jit(solution)/shard_map/ppermute | solution.py:23
  22.5 38.9 %collective-permute-start.1 = (bf16[2,128,48,128]{3,2,1,0:T(8,128)(2,1)}, bf16[2,128,48,128]{3,2,1,0:T(8,128)(2,1)}, u32[]{:S(2)}, u32[]{:S(2)}) collective-permute-start(bf16[2,128,48,128]{3,2,1,0:T(8,128)(2,1)} %fusion.9), channel_id=1, source_target_pairs={{1,0},{2,1},{3,2},{4,3},{5,4},{6,5},{7,6},{9,8},{10,9},{11,10},{12... | collective-permute-start | bytes 9437192 | tf_op jit(solution)/shard_map/ppermute | solution.py:24
  24.5 18.6 %collective-permute-start.3 = (s32[16]{0:T(128)S(1)}, s32[16]{0:T(128)S(1)}, u32[]{:S(2)}, u32[]{:S(2)}) collective-permute-start(s32[16]{0:T(128)S(1)} %get-tuple-element.27), channel_id=1, source_target_pairs={{8,0},{16,8},{24,16},{32,24},{40,32},{48,40},{56,48},{64,56},{72,6... | collective-permute-start | bytes 200 | tf_op jit(solution)/shard_map/ppermute | solution.py:59
  25.8 17.3 %collective-permute-start.2 = (s32[16]{0:T(128)S(1)}, s32[16]{0:T(128)S(1)}, u32[]{:S(2)}, u32[]{:S(2)}) collective-permute-start(s32[16]{0:T(128)S(1)} %get-tuple-element.26), channel_id=1, source_target_pairs={{0,8},{8,16},{16,24},{24,32},{32,40},{40,48},{48,56},{56,64},{64,7... | collective-permute-start | bytes 200 | tf_op jit(solution)/shard_map/ppermute | solution.py:58
Sparse Core Ops, SparseCore 0:
  124.2 95.7 reduce-scatter.3

commit v6 on v5

--- a/solution.py
+++ b/solution.py
@@ -65,9 +65,14 @@
 
 def on_device(spectra, segment_ids, pair_blocks, pair_count):
     weight = window_weight(segment_ids)
-    whitened = whiten_transposed(spectra)
-    block_count = whitened.shape[0]
-    extended = padded(whitened, (("tile", 0),), block_count)
+    block_count = spectra.shape[1]
+    pieces = [whiten_transposed(spectra[:, i : i + 1]) for i in range(block_count)]
+    count = lax.axis_size("tile")
+    up = [(i, i + 1) for i in range(count - 1)]
+    down = [(j, i) for i, j in up]
+    before = [lax.ppermute(piece, "tile", up) for piece in pieces]
+    after = [lax.ppermute(piece, "tile", down) for piece in pieces]
+    extended = jnp.concatenate(before + pieces + after, axis=0)
     first_local = lax.axis_index("tile") * block_count - block_count
     basis = lag_table().reshape(2, FB, LAGS)
     slot_total = pair_blocks.shape[0]

time: 227 us -> 223 us (0.982)
  waiting for transfers between devices: 114 us -> 101 us
  local copies, waits for them, and re-layouts: 10.9 us -> 20.4 us
  other arithmetic: 18.8 us -> 12.6 us
  starting transfers between devices: 12.1 us -> 17.8 us
    ppermute x2 -> x4, waiting for transfers between devices: 18 us -> 0.01 us  [the longest x2 0.01 us: on_device(): before = [lax.ppermute(piece, 'tile', up) for piece in pieces]]
    unnamed x5 -> x11, local copies, waits for them, and re-layouts: 3.7 us -> 9.61 us
    ppermute x2 -> x4, starting transfers between devices: 6.83 us -> 12.4 us  [the longest x2 8.55 us: on_device(): before = [lax.ppermute(piece, 'tile', up) for piece in pieces]]
    concatenate x1 -> x0, other arithmetic: 4.64 us -> none  [padded(): value = jnp.concatenate([before, value, after], axis=dim)]
    unnamed x2, waiting for transfers between devices: 95.9 us -> 100 us
    slice x0 -> x1, local copies, waits for them, and re-layouts: none -> 3.37 us  [on_device(): spectra[:, i:i + 1]]
  transfers between devices with their start and end apart: 5 -> 7, of which waited for: 3 -> 2; matrix products, arithmetic and copies ran while one was open for 1% -> 7% of each run, Pallas kernels for 0% -> 0%
where the time goes in v6:
time: 223 us
  waiting for transfers between devices  101 us (45%)
  matrix products  45.3 us (20%)
  between operations  25.9 us (12%)
  local copies, waits for them, and re-layouts  20.4 us (9%)
  starting transfers between devices  17.8 us (8%)
  other arithmetic  12.6 us (6%)
    unnamed x2, waiting for transfers between devices  100 us
    dot_general x1, matrix products, on_device(): jnp.einsum('skqgcd,qkl->gscld', cross, basis, precision=lax.Precision.HIGH)  32.9 us
    dot_general x1, matrix products, on_device(): jnp.einsum('qpskwc,pskwd->skqcd', left_both, right_both, preferred_elemen...  12.5 us
    unnamed x11, local copies, waits for them, and re-layouts  9.61 us
    ppermute x2, starting transfers between devices, on_device(): before = [lax.ppermute(piece, 'tile', up) for piece in pieces]  8.55 us
  transfers between devices with their start and end apart: 7, of which 2 were waited for; matrix products, arithmetic and copies ran while one was open for 7% of the time, Pallas kernels for 0%

profile of v6, /device:TPU:1, one launch (start us, length us, event | category | flops | bytes accessed | tf_op | source)
XLA Modules:
  0.0 222.9 jit_solution(3157291292803197358)
XLA Ops:
  6.5 3.4 %fusion.20 = (bf16[48,1,128,128]{3,2,1,0:T(8,128)(2,1)}, bf16[48,1,128,128]{3,2,1,0:T(8,128)(2,1)S(1)}) fusion(bf16[48,2,128,128]{3,2,1,0:T(8,128)(2,1)} %param.4), kind=kLoop, calls=%fused_computation.68 | loop fusion | bytes 6291456 | tf_op jit(solution)/shard_map/slice | solution.py:69
  9.9 1.0 copy.41
  10.9 0.2 convert_element_type.34
  11.6 0.3 fusion.11
  11.9 4.9 %collective-permute-start = (bf16[1,128,48,128]{3,2,1,0:T(8,128)(2,1)S(1)}, bf16[1,128,48,128]{3,2,1,0:T(8,128)(2,1)}, u32[]{:S(2)}, u32[]{:S(2)}) collective-permute-start(bf16[1,128,48,128]{3,2,1,0:T(8,128)(2,1)S(1)} %fusion.11), channel_id=1, source_target_pairs={{0,1},{1,2},{2,3},{3,4},{4,5},{5,6},{6,7},{8,9},{9,10},{10,11},{11... | collective-permute-start | bytes 4718600 | tf_op jit(solution)/shard_map/ppermute | solution.py:73
  16.9 1.9 collective-permute-start.2
  18.8 2.0 copy.42
  20.8 0.2 convert_element_type.36
  21.1 1.4 fusion.12
  22.4 1.5 reduce_sum.28
  24.1 1.5 fusion.10
  25.6 3.6 %collective-permute-start.1 = (bf16[1,128,48,128]{3,2,1,0:T(8,128)(2,1)}, bf16[1,128,48,128]{3,2,1,0:T(8,128)(2,1)}, u32[]{:S(2)}, u32[]{:S(2)}) collective-permute-start(bf16[1,128,48,128]{3,2,1,0:T(8,128)(2,1)} %fusion.10), channel_id=1, source_target_pairs={{0,1},{1,2},{2,3},{3,4},{4,5},{5,6},{6,7},{8,9},{9,10},{10,11},{11... | collective-permute-start | bytes 4718600 | tf_op jit(solution)/shard_map/ppermute | solution.py:73
  29.2 1.9 collective-permute-start.3
  31.2 1.3 collective-permute-start.5
  32.5 0.7 fusion.21
  40.9 0.2 fusion.18
  45.8 4.2 %collective-permute-start.4 = (s32[16]{0:T(128)S(1)}, s32[16]{0:T(128)S(1)}, u32[]{:S(2)}, u32[]{:S(2)}) collective-permute-start(s32[16]{0:T(128)S(1)} %get-tuple-element.28), channel_id=1, source_target_pairs={{0,8},{8,16},{16,24},{24,32},{32,40},{40,48},{48,56},{56,64},{64,7... | collective-permute-start | bytes 200 | tf_op jit(solution)/shard_map/ppermute | solution.py:58
  50.0 0.5 collective-permute-done.4
  50.8 1.5 constant_dynamic-update-slice_fusion.5
  52.3 1.6 constant_dynamic-update-slice_fusion.4
  53.9 0.2 constant_dynamic-update-slice_fusion.3
  54.2 1.6 constant_dynamic-update-slice_fusion.2
  55.8 1.6 constant_dynamic-update-slice_fusion.1
  57.6 3.3 %constant_dynamic-slice_fusion.2 = (bf16[1,128,48,128]{3,2,1,0:T(8,128)(2,1)S(1)}, bf16[1,128,48,128]{3,2,1,0:T(8,128)(2,1)S(1)}, bf16[1,128,48,128]{3,2,1,0:T(8...) fusion(bf16[6,128,48,128]{3,2,1,0:T(8,128)(2,1)S(1)} %constant_, ...), kind=kLoop, calls=%fused_computation.55 | loop fusion | bytes 18874392 | tf_op jit(solution)/shard_map/jit(dynamic_index_in_dim)/dynamic_slice | solution.py:86
  60.9 2.5 %multiply_convert_fusion = bf16[3,128,48,128]{3,2,1,0:T(8,128)(2,1)S(1)} fusion(bf16[1,128,48,128]{3,2,1,0:T(8,128)(2,1)S(1)} %get-tuple-element.8, bf16[1,128,48,128]{3,2,1,0:T(8,128)(2,1)} %get-tuple-element.9, bf16[1,128,48,128]{3,2,1,0:T(8,128)(2,1)} %get-tuple-element.10, f32[48]{0:T(128)S(1)} %broadcast_divide_fusion), kind=kLoop, calls=%fused_computation.7 | loop fusion | flops 11796480 | bytes 9437376 | tf_op jit(solution)/shard_map/convert_element_type | solution.py:88
  63.4 0.6 slice_bitcast_fusion.3
  64.1 0.6 pad_maximum_fusion.1
  64.6 2.9 %slice_bitcast_fusion.1 = (bf16[1,3,64,48,128]{4,3,0,2,1:T(8,128)(2,1)}, bf16[1,3,64,48,128]{4,3,0,2,1:T(8,128)(2,1)}) fusion(bf16[3,128,48,128]{3,2,1,0:T(8,128)(2,1)S(1)} %pad_maximum_fusion.1), kind=kLoop, calls=%fused_computation.19 | loop fusion | bytes 9437184 | tf_op jit(solution)/shard_map/stack | solution.py:92
  67.5 2.9 %maximum_bitcast_fusion = (bf16[1,2,3,64,48,128]{5,4,3,2,1,0:T(8,128)(2,1)S(1)}, bf16[1,2,3,64,48,128]{5,4,3,2,1,0:T(8,128)(2,1)}) fusion(bf16[1,3,64,48,128]{4,3,2,1,0:T(8,128)(2,1)S(1)} %get-tuple-element.15, bf16[1,3,64,48,128]{4,3,2,1,0:T(8,128)(2,1)S(1)} %get-tuple-element.13, bf16[1,3,64,48,128]{4,3,2,1,0:T(8,128)(2,1)S(1)} %get-tuple-element.14), kind=kLoop, calls=%fused_computation.8 | loop fusion | flops 4718592 | bytes 16515072 | tf_op jit(solution)/shard_map/stack | solution.py:91
  70.4 12.5 %convolution_bitcast_fusion = f32[3,64,2,16,8,128]{5,4,3,2,1,0:T(8,128)} fusion(bf16[1,3,64,48,128]{4,3,0,2,1:T(8,128)(2,1)} %get-tuple-element.12, bf16[1,3,64,48,128]{4,3,0,2,1:T(8,128)(2,1)} %get-tuple-element.11, bf16[1,2,3,64,48,128]{5,4,3,2,1,0:T(8,128)(2,1)} %get-tuple-element.19, bf16[1,2,3,64,48,128]{5,4,3,2,1,0:T(8,128)(2,1)S(1)} %get-tuple-element.18), kind=kOutput, calls=%fused_computation.4 | convolution fusion | flops 1215037440 | bytes 39321600 | tf_op jit(solution)/shard_map/qpskwc,pskwd->skqcd/dot_general | solution.py:93
  82.9 32.9 %fusion.2 = f32[16,3,8,64,128]{4,3,2,1,0:T(8,128)} fusion(f32[3]{0:T(128)S(1)} %compare_convert_fusion, f32[3,64,2,16,8,128]{5,4,3,2,1,0:T(8,128)} %convolution_bitcast_fusion, f32[2,64,64,1,1,1]{1,0,2,5,4,3:T(2,128)S(1)} %bitcast.57), kind=kOutput, calls=%fused_computation.3 | convolution fusion | flops 2419064832 | bytes 37781516 | tf_op jit(solution)/shard_map/skqgcd,qkl->gscld/dot_general | solution.py:99
  115.7 100.3 %reduce-scatter.4.cloned.1.call-done = f32[1,3,8,64,128]{4,3,2,1,0:T(8,128)} async-done(((f32[16,3,8,64,128]{4,3,2,1,0:T(8,128)}), f32[1,3,8,64,128]{4,3,2,1,0:T(8,128)}) %reduce-scatter.4.cloned.1.call-update) | async-done | bytes 786448
  (30 shorter events, 1.3 us)
Async XLA Ops:
  6.5 209.5 %reduce-scatter.4.cloned.1.call-start = ((), (), s32[]{:S(2)}) async-start(), calls=%async_computation.1 | async-start | bytes 13369344
  11.9 38.9 %collective-permute-start = (bf16[1,128,48,128]{3,2,1,0:T(8,128)(2,1)S(1)}, bf16[1,128,48,128]{3,2,1,0:T(8,128)(2,1)}, u32[]{:S(2)}, u32[]{:S(2)}) collective-permute-start(bf16[1,128,48,128]{3,2,1,0:T(8,128)(2,1)S(1)} %fusion.11), channel_id=1, source_target_pairs={{0,1},{1,2},{2,3},{3,4},{4,5},{5,6},{6,7},{8,9},{9,10},{10,11},{11... | collective-permute-start | bytes 4718600 | tf_op jit(solution)/shard_map/ppermute | solution.py:73
  16.9 38.9 %collective-permute-start.2 = (bf16[1,128,48,128]{3,2,1,0:T(8,128)(2,1)S(1)}, bf16[1,128,48,128]{3,2,1,0:T(8,128)(2,1)}, u32[]{:S(2)}, u32[]{:S(2)}) collective-permute-start(bf16[1,128,48,128]{3,2,1,0:T(8,128)(2,1)S(1)} %fusion.11), channel_id=1, source_target_pairs={{1,0},{2,1},{3,2},{4,3},{5,4},{6,5},{7,6},{9,8},{10,9},{11,10},{12... | collective-permute-start | bytes 4718600 | tf_op jit(solution)/shard_map/ppermute | solution.py:74
  23.9 7.2 %copy-start.1 = (s32[48]{0:T(128)S(1)}, s32[48]{0:T(128)}, u32[]{:S(2)}) copy-start(s32[48]{0:T(128)} %param.5) | copy-start | bytes 580
  24.0 8.6 %copy-start = (s32[3,2]{0,1:T(2,128)S(1)}, s32[3,2]{0,1:T(2,128)}, u32[]{:S(2)}) copy-start(s32[3,2]{0,1:T(2,128)} %param.6) | copy-start | bytes 76
  25.6 26.8 %collective-permute-start.1 = (bf16[1,128,48,128]{3,2,1,0:T(8,128)(2,1)}, bf16[1,128,48,128]{3,2,1,0:T(8,128)(2,1)}, u32[]{:S(2)}, u32[]{:S(2)}) collective-permute-start(bf16[1,128,48,128]{3,2,1,0:T(8,128)(2,1)} %fusion.10), channel_id=1, source_target_pairs={{0,1},{1,2},{2,3},{3,4},{4,5},{5,6},{6,7},{8,9},{9,10},{10,11},{11... | collective-permute-start | bytes 4718600 | tf_op jit(solution)/shard_map/ppermute | solution.py:73
  29.2 28.2 %collective-permute-start.3 = (bf16[1,128,48,128]{3,2,1,0:T(8,128)(2,1)}, bf16[1,128,48,128]{3,2,1,0:T(8,128)(2,1)S(1)}, u32[]{:S(2)}, u32[]{:S(2)}) collective-permute-start(bf16[1,128,48,128]{3,2,1,0:T(8,128)(2,1)} %fusion.10), channel_id=1, source_target_pairs={{1,0},{2,1},{3,2},{4,3},{5,4},{6,5},{7,6},{9,8},{10,9},{11,10},{12... | collective-permute-start | bytes 4718600 | tf_op jit(solution)/shard_map/ppermute | solution.py:74
  31.2 14.6 %collective-permute-start.5 = (s32[16]{0:T(128)S(1)}, s32[16]{0:T(128)S(1)}, u32[]{:S(2)}, u32[]{:S(2)}) collective-permute-start(s32[16]{0:T(128)S(1)} %get-tuple-element.29), channel_id=1, source_target_pairs={{8,0},{16,8},{24,16},{32,24},{40,32},{48,40},{56,48},{64,56},{72,6... | collective-permute-start | bytes 200 | tf_op jit(solution)/shard_map/ppermute | solution.py:59
  45.8 4.7 %collective-permute-start.4 = (s32[16]{0:T(128)S(1)}, s32[16]{0:T(128)S(1)}, u32[]{:S(2)}, u32[]{:S(2)}) collective-permute-start(s32[16]{0:T(128)S(1)} %get-tuple-element.28), channel_id=1, source_target_pairs={{0,8},{8,16},{16,24},{24,32},{32,40},{40,48},{48,56},{56,64},{64,7... | collective-permute-start | bytes 200 | tf_op jit(solution)/shard_map/ppermute | solution.py:58
Sparse Core Ops, SparseCore 0:
  115.9 100.0 reduce-scatter.3

commit v7 on v6

--- a/solution.py
+++ b/solution.py
@@ -65,6 +65,7 @@
 
 def on_device(spectra, segment_ids, pair_blocks, pair_count):
     weight = window_weight(segment_ids)
+    spectra, weight = lax.optimization_barrier((spectra, weight))
     block_count = spectra.shape[1]
     pieces = [whiten_transposed(spectra[:, i : i + 1]) for i in range(block_count)]
     count = lax.axis_size("tile")

time: 223 us -> 239 us (1.072)
  waiting for transfers between devices: 101 us -> 114 us
  other arithmetic: 12.6 us -> 16.7 us
  local copies, waits for them, and re-layouts: 20.4 us -> 17.7 us
    ppermute x2, waiting for transfers between devices: 0.01 us -> 13.8 us  [on_device(): before = [lax.ppermute(piece, 'tile', up) for piece in pieces]]
    unnamed x11 -> x7, local copies, waits for them, and re-layouts: 9.61 us -> 5.15 us
    optimization_barrier x0 -> x1, local copies, waits for them, and re-layouts: none -> 3.7 us  [on_device(): spectra, weight = lax.optimization_barrier((spectra, weight))]
    slice x1 -> x0, local copies, waits for them, and re-layouts: 3.37 us -> none  [on_device(): spectra[:, i:i + 1]]
  transfers between devices with their start and end apart: 7 -> 7, of which waited for: 2 -> 4; matrix products, arithmetic and copies ran while one was open for 7% -> 3% of each run, Pallas kernels for 0% -> 0%
where the time goes in v7:
time: 239 us; the launch traced here: 238 us
  waiting for transfers between devices  114 us (48%)
  matrix products  45.3 us (19%)
  between operations  25.7 us (11%)
  starting transfers between devices  18.7 us (8%)
  local copies, waits for them, and re-layouts  17.7 us (7%)
  other arithmetic  16.7 us (7%)
    unnamed x2, waiting for transfers between devices  98.2 us
    dot_general x1, matrix products, on_device(): jnp.einsum('skqgcd,qkl->gscld', cross, basis, precision=lax.Precision.HIGH)  32.9 us
    ppermute x2, waiting for transfers between devices, on_device(): before = [lax.ppermute(piece, 'tile', up) for piece in pieces]  13.8 us
    dot_general x1, matrix products, on_device(): jnp.einsum('qpskwc,pskwd->skqcd', left_both, right_both, preferred_elemen...  12.5 us
    ppermute x2, starting transfers between devices, on_device(): before = [lax.ppermute(piece, 'tile', up) for piece in pieces]  7.39 us
    ppermute x2, starting transfers between devices, on_device(): after = [lax.ppermute(piece, 'tile', down) for piece in pieces]  5.47 us
    unnamed x7, local copies, waits for them, and re-layouts  5.15 us
  transfers between devices with their start and end apart: 7, of which 4 were waited for; matrix products, arithmetic and copies ran while one was open for 3% of the time, Pallas kernels for 0%

profile of v7, /device:TPU:1, one launch (start us, length us, event | category | flops | bytes accessed | tf_op | source)
XLA Modules:
  0.0 238.4 jit_solution(2710546810114764392)
XLA Ops:
  6.5 0.7 broadcast_add_fusion.2
  7.3 1.3 collective-permute-start.1
  8.6 4.6 %collective-permute-start = (s32[16]{0:T(128)S(1)}, s32[16]{0:T(128)S(1)}, u32[]{:S(2)}, u32[]{:S(2)}) collective-permute-start(s32[16]{0:T(128)S(1)} %get-tuple-element.34), channel_id=1, source_target_pairs={{0,8},{8,16},{16,24},{24,32},{32,40},{40,48},{48,56},{56,64},{64,7... | collective-permute-start | bytes 200 | tf_op jit(solution)/shard_map/ppermute | solution.py:58
  13.1 0.7 collective-permute-done
  13.8 0.7 pad_add_fusion
  14.6 0.8 convert_reduce_fusion
  15.4 3.7 %copy.25 = bf16[48,2,128,128]{2,0,3,1:T(8,128)(2,1)S(1)} copy(bf16[48,2,128,128]{3,2,1,0:T(8,128)(2,1)} %param.4) | data formatting | bytes 6291456 | tf_op jit(solution)/shard_map/optimization_barrier | solution.py:68
  19.1 0.5 slice_convert_fusion
  19.6 2.0 fusion.12
  21.6 1.5 reduce_sum.28
  23.2 1.5 reduce_sum.29
  24.9 2.1 fusion.10
  27.0 5.5 %collective-permute-start.2 = (bf16[1,128,48,128]{3,2,1,0:T(8,128)(2,1)}, bf16[1,128,48,128]{3,2,1,0:T(8,128)(2,1)S(1)}, u32[]{:S(2)}, u32[]{:S(2)}) collective-permute-start(bf16[1,128,48,128]{3,2,1,0:T(8,128)(2,1)} %get-tuple-element.21), channel_id=1, source_target_pairs={{0,1},{1,2},{2,3},{3,4},{4,5},{5,6},{6,7},{8,9},{9,10},{10,11},{11... | collective-permute-start | bytes 4718600 | tf_op jit(solution)/shard_map/ppermute | solution.py:74
  32.5 1.9 collective-permute-start.3
  34.4 3.6 %collective-permute-start.4 = (bf16[1,128,48,128]{3,2,1,0:T(8,128)(2,1)}, bf16[1,128,48,128]{3,2,1,0:T(8,128)(2,1)S(1)}, u32[]{:S(2)}, u32[]{:S(2)}) collective-permute-start(bf16[1,128,48,128]{3,2,1,0:T(8,128)(2,1)} %get-tuple-element.21), channel_id=1, source_target_pairs={{1,0},{2,1},{3,2},{4,3},{5,4},{6,5},{7,6},{9,8},{10,9},{11,10},{12... | collective-permute-start | bytes 4718600 | tf_op jit(solution)/shard_map/ppermute | solution.py:75
  38.0 1.9 collective-permute-start.5
  39.9 0.7 fusion.20
  53.2 13.8 %collective-permute-done.3 = bf16[1,128,48,128]{3,2,1,0:T(8,128)(2,1)} collective-permute-done((bf16[1,128,48,128]{3,2,1,0:T(8,128)(2,1)}, bf16[1,128,48,128]{3,2,1,0:T(8,128)(2,1)}, u32[]{:S(2)}, u32[]{:S(2)}) %collective-permute-start.3) | collective-permute-done | bytes 1572896 | tf_op jit(solution)/shard_map/ppermute | solution.py:74
  67.0 1.6 constant_dynamic-update-slice_fusion.4
  68.6 1.6 constant_dynamic-update-slice_fusion.3
  70.2 1.6 constant_dynamic-update-slice_fusion.2
  72.1 1.5 collective-permute-done.5
  73.6 1.6 constant_dynamic-update-slice_fusion
  75.2 3.3 %constant_dynamic-slice_fusion.2 = (bf16[1,128,48,128]{3,2,1,0:T(8,128)(2,1)S(1)}, bf16[1,128,48,128]{3,2,1,0:T(8,128)(2,1)S(1)}, bf16[1,128,48,128]{3,2,1,0:T(8...) fusion(bf16[6,128,48,128]{3,2,1,0:T(8,128)(2,1)S(1)} %constant_, ...), kind=kLoop, calls=%fused_computation.57 | loop fusion | bytes 18874392 | tf_op jit(solution)/shard_map/jit(dynamic_index_in_dim)/dynamic_slice | solution.py:87
  78.5 2.5 %multiply_convert_fusion = bf16[3,128,48,128]{3,2,1,0:T(8,128)(2,1)S(1)} fusion(bf16[1,128,48,128]{3,2,1,0:T(8,128)(2,1)S(1)} %get-tuple-element.12, bf16[1,128,48,128]{3,2,1,0:T(8,128)(2,1)} %get-tuple-element.13, bf16[1,128,48,128]{3,2,1,0:T(8,128)(2,1)} %get-tuple-element.14, f32[48]{0:T(128)S(1)} %broadcast_divide_fusion), kind=kLoop, calls=%fused_computation.7 | loop fusion | flops 11796480 | bytes 9437376 | tf_op jit(solution)/shard_map/convert_element_type | solution.py:89
  81.0 0.6 slice_bitcast_fusion.3
  81.6 0.6 pad_maximum_fusion.1
  82.2 2.9 %slice_bitcast_fusion.1 = (bf16[1,3,64,48,128]{4,3,0,2,1:T(8,128)(2,1)}, bf16[1,3,64,48,128]{4,3,0,2,1:T(8,128)(2,1)}) fusion(bf16[3,128,48,128]{3,2,1,0:T(8,128)(2,1)S(1)} %pad_maximum_fusion.1), kind=kLoop, calls=%fused_computation.19 | loop fusion | bytes 9437184 | tf_op jit(solution)/shard_map/stack | solution.py:93
  85.1 2.9 %maximum_bitcast_fusion = (bf16[1,2,3,64,48,128]{5,4,3,2,1,0:T(8,128)(2,1)S(1)}, bf16[1,2,3,64,48,128]{5,4,3,2,1,0:T(8,128)(2,1)}) fusion(bf16[1,3,64,48,128]{4,3,2,1,0:T(8,128)(2,1)S(1)} %get-tuple-element.19, bf16[1,3,64,48,128]{4,3,2,1,0:T(8,128)(2,1)S(1)} %get-tuple-element.17, bf16[1,3,64,48,128]{4,3,2,1,0:T(8,128)(2,1)S(1)} %get-tuple-element.18), kind=kLoop, calls=%fused_computation.8 | loop fusion | flops 4718592 | bytes 16515072 | tf_op jit(solution)/shard_map/stack | solution.py:92
  88.0 12.5 %convolution_bitcast_fusion = f32[3,64,2,16,8,128]{5,4,3,2,1,0:T(8,128)} fusion(bf16[1,3,64,48,128]{4,3,0,2,1:T(8,128)(2,1)} %get-tuple-element.16, bf16[1,3,64,48,128]{4,3,0,2,1:T(8,128)(2,1)} %get-tuple-element.15, bf16[1,2,3,64,48,128]{5,4,3,2,1,0:T(8,128)(2,1)} %get-tuple-element.25, bf16[1,2,3,64,48,128]{5,4,3,2,1,0:T(8,128)(2,1)S(1)} %get-tuple-element.24), kind=kOutput, calls=%fused_computation.4 | convolution fusion | flops 1215037440 | bytes 39321600 | tf_op jit(solution)/shard_map/qpskwc,pskwd->skqcd/dot_general | solution.py:94
  100.4 32.9 %fusion.2 = f32[16,3,8,64,128]{4,3,2,1,0:T(8,128)} fusion(f32[3]{0:T(128)S(1)} %compare_convert_fusion, f32[3,64,2,16,8,128]{5,4,3,2,1,0:T(8,128)} %convolution_bitcast_fusion, f32[2,64,64,1,1,1]{1,0,2,5,4,3:T(2,128)S(1)} %bitcast.57), kind=kOutput, calls=%fused_computation.3 | convolution fusion | flops 2419064832 | bytes 37781516 | tf_op jit(solution)/shard_map/skqgcd,qkl->gscld/dot_general | solution.py:100
  133.3 98.2 %reduce-scatter.4.cloned.1.call-done = f32[1,3,8,64,128]{4,3,2,1,0:T(8,128)} async-done(((f32[16,3,8,64,128]{4,3,2,1,0:T(8,128)}), f32[1,3,8,64,128]{4,3,2,1,0:T(8,128)}) %reduce-scatter.4.cloned.1.call-update) | async-done | bytes 786448
  (23 shorter events, 1.1 us)
Async XLA Ops:
  6.5 225.0 %reduce-scatter.4.cloned.1.call-start = ((), (), s32[]{:S(2)}) async-start(), calls=%async_computation.1 | async-start | bytes 13369344
  7.3 5.9 %collective-permute-start.1 = (s32[16]{0:T(128)S(1)}, s32[16]{0:T(128)S(1)}, u32[]{:S(2)}, u32[]{:S(2)}) collective-permute-start(s32[16]{0:T(128)S(1)} %get-tuple-element.35), channel_id=1, source_target_pairs={{8,0},{16,8},{24,16},{32,24},{40,32},{48,40},{56,48},{64,56},{72,6... | collective-permute-start | bytes 200 | tf_op jit(solution)/shard_map/ppermute | solution.py:59
  8.6 5.3 %collective-permute-start = (s32[16]{0:T(128)S(1)}, s32[16]{0:T(128)S(1)}, u32[]{:S(2)}, u32[]{:S(2)}) collective-permute-start(s32[16]{0:T(128)S(1)} %get-tuple-element.34), channel_id=1, source_target_pairs={{0,8},{8,16},{16,24},{24,32},{32,40},{40,48},{48,56},{56,64},{64,7... | collective-permute-start | bytes 200 | tf_op jit(solution)/shard_map/ppermute | solution.py:58
  24.9 15.0 %copy-start = (s32[3,2]{0,1:T(2,128)S(1)}, s32[3,2]{0,1:T(2,128)}, u32[]{:S(2)}) copy-start(s32[3,2]{0,1:T(2,128)} %param.6) | copy-start | bytes 76
  27.0 26.0 %collective-permute-start.2 = (bf16[1,128,48,128]{3,2,1,0:T(8,128)(2,1)}, bf16[1,128,48,128]{3,2,1,0:T(8,128)(2,1)S(1)}, u32[]{:S(2)}, u32[]{:S(2)}) collective-permute-start(bf16[1,128,48,128]{3,2,1,0:T(8,128)(2,1)} %get-tuple-element.21), channel_id=1, source_target_pairs={{0,1},{1,2},{2,3},{3,4},{4,5},{5,6},{6,7},{8,9},{9,10},{10,11},{11... | collective-permute-start | bytes 4718600 | tf_op jit(solution)/shard_map/ppermute | solution.py:74
  32.5 34.5 %collective-permute-start.3 = (bf16[1,128,48,128]{3,2,1,0:T(8,128)(2,1)}, bf16[1,128,48,128]{3,2,1,0:T(8,128)(2,1)}, u32[]{:S(2)}, u32[]{:S(2)}) collective-permute-start(bf16[1,128,48,128]{3,2,1,0:T(8,128)(2,1)} %get-tuple-element.20), channel_id=1, source_target_pairs={{0,1},{1,2},{2,3},{3,4},{4,5},{5,6},{6,7},{8,9},{9,10},{10,11},{11... | collective-permute-start | bytes 4718600 | tf_op jit(solution)/shard_map/ppermute | solution.py:74
  34.4 37.4 %collective-permute-start.4 = (bf16[1,128,48,128]{3,2,1,0:T(8,128)(2,1)}, bf16[1,128,48,128]{3,2,1,0:T(8,128)(2,1)S(1)}, u32[]{:S(2)}, u32[]{:S(2)}) collective-permute-start(bf16[1,128,48,128]{3,2,1,0:T(8,128)(2,1)} %get-tuple-element.21), channel_id=1, source_target_pairs={{1,0},{2,1},{3,2},{4,3},{5,4},{6,5},{7,6},{9,8},{10,9},{11,10},{12... | collective-permute-start | bytes 4718600 | tf_op jit(solution)/shard_map/ppermute | solution.py:75
  38.0 35.6 %collective-permute-start.5 = (bf16[1,128,48,128]{3,2,1,0:T(8,128)(2,1)}, bf16[1,128,48,128]{3,2,1,0:T(8,128)(2,1)}, u32[]{:S(2)}, u32[]{:S(2)}) collective-permute-start(bf16[1,128,48,128]{3,2,1,0:T(8,128)(2,1)} %get-tuple-element.20), channel_id=1, source_target_pairs={{1,0},{2,1},{3,2},{4,3},{5,4},{6,5},{7,6},{9,8},{10,9},{11,10},{12... | collective-permute-start | bytes 4718600 | tf_op jit(solution)/shard_map/ppermute | solution.py:75
Sparse Core Ops, SparseCore 0:
  133.4 98.0 reduce-scatter.3

commit v8 on v6

--- a/solution.py
+++ b/solution.py
@@ -66,12 +66,19 @@
 def on_device(spectra, segment_ids, pair_blocks, pair_count):
     weight = window_weight(segment_ids)
     block_count = spectra.shape[1]
-    pieces = [whiten_transposed(spectra[:, i : i + 1]) for i in range(block_count)]
     count = lax.axis_size("tile")
     up = [(i, i + 1) for i in range(count - 1)]
     down = [(j, i) for i, j in up]
-    before = [lax.ppermute(piece, "tile", up) for piece in pieces]
-    after = [lax.ppermute(piece, "tile", down) for piece in pieces]
+    raw = spectra[:, 0:1]
+    raw_before = lax.ppermute(raw, "tile", up)
+    raw_after = lax.ppermute(raw, "tile", down)
+    pieces = [whiten_transposed(spectra[:, i : i + 1]) for i in range(block_count)]
+    before = [whiten_transposed(raw_before)] + [
+        lax.ppermute(piece, "tile", up) for piece in pieces[1:]
+    ]
+    after = [whiten_transposed(raw_after)] + [
+        lax.ppermute(piece, "tile", down) for piece in pieces[1:]
+    ]
     extended = jnp.concatenate(before + pieces + after, axis=0)
     first_local = lax.axis_index("tile") * block_count - block_count
     basis = lag_table().reshape(2, FB, LAGS)

time: 223 us -> 230 us (1.031)
  other arithmetic: 12.6 us -> 20.1 us
    unnamed x0 -> x3, other arithmetic: none -> 4.01 us
    convert_element_type x2 -> x4, other arithmetic: 0.46 us -> 3.74 us  [whiten_transposed(): values = spectra.astype(jnp.float32)]
    unnamed x11 -> x8, local copies, waits for them, and re-layouts: 9.61 us -> 6.43 us
  transfers between devices with their start and end apart: 7 -> 7, of which waited for: 2 -> 2; matrix products, arithmetic and copies ran while one was open for 7% -> 9% of each run, Pallas kernels for 0% -> 0%
where the time goes in v8:
time: 230 us; the launch traced here: 229 us
  waiting for transfers between devices  101 us (44%)
  matrix products  45.3 us (20%)
  between operations  26 us (11%)
  other arithmetic  20.1 us (9%)
  local copies, waits for them, and re-layouts  18.9 us (8%)
  starting transfers between devices  17.8 us (8%)
    unnamed x2, waiting for transfers between devices  100 us
    dot_general x1, matrix products, on_device(): jnp.einsum('skqgcd,qkl->gscld', cross, basis, precision=lax.Precision.HIGH)  32.8 us
    dot_general x1, matrix products, on_device(): jnp.einsum('qpskwc,pskwd->skqcd', left_both, right_both, preferred_elemen...  12.4 us
    unnamed x8, local copies, waits for them, and re-layouts  6.43 us
    ppermute x1, starting transfers between devices, on_device(): raw_before = lax.ppermute(raw, 'tile', up)  4.93 us
  transfers between devices with their start and end apart: 7, of which 2 were waited for; matrix products, arithmetic and copies ran while one was open for 9% of the time, Pallas kernels for 0%

profile of v8, /device:TPU:1, one launch (start us, length us, event | category | flops | bytes accessed | tf_op | source)
XLA Modules:
  0.0 229.1 jit_solution(16858776611377313703)
XLA Ops:
  6.5 3.4 %fusion.29 = (bf16[48,1,128,128]{3,2,1,0:T(8,128)(2,1)}, bf16[48,1,128,128]{3,2,1,0:T(8,128)(2,1)S(1)}) fusion(bf16[48,2,128,128]{3,2,1,0:T(8,128)(2,1)} %param.4), kind=kLoop, calls=%fused_computation.82 | loop fusion | bytes 6291456 | tf_op jit(solution)/shard_map/slice | solution.py:75
  9.9 1.0 copy.41
  10.9 4.9 %collective-permute-start = (bf16[48,1,128,128]{2,0,3,1:T(8,128)(2,1)S(1)}, bf16[48,1,128,128]{2,0,3,1:T(8,128)(2,1)}, u32[]{:S(2)}, u32[]{:S(2)}) collective-permute-start(bf16[48,1,128,128]{2,0,3,1:T(8,128)(2,1)S(1)} %copy.41), channel_id=1, source_target_pairs={{0,1},{1,2},{2,3},{3,4},{4,5},{5,6},{6,7},{8,9},{9,10},{10,11},{11... | collective-permute-start | bytes 4718600 | tf_op jit(solution)/shard_map/ppermute | solution.py:73
  15.9 1.9 collective-permute-start.2
  17.8 2.0 copy.42
  19.8 0.2 convert_element_type.48
  20.1 1.3 fusion.21
  21.4 1.5 reduce_sum.46
  23.0 1.5 fusion.16
  24.5 3.6 %collective-permute-start.1 = (bf16[1,128,48,128]{3,2,1,0:T(8,128)(2,1)}, bf16[1,128,48,128]{3,2,1,0:T(8,128)(2,1)}, u32[]{:S(2)}, u32[]{:S(2)}) collective-permute-start(bf16[1,128,48,128]{3,2,1,0:T(8,128)(2,1)} %fusion.16), channel_id=1, source_target_pairs={{0,1},{1,2},{2,3},{3,4},{4,5},{5,6},{6,7},{8,9},{9,10},{10,11},{11... | collective-permute-start | bytes 4718600 | tf_op jit(solution)/shard_map/ppermute | solution.py:77
  28.2 1.9 collective-permute-start.3
  30.2 1.3 collective-permute-start.5
  32.4 0.7 fusion.30
  45.5 4.2 %collective-permute-start.4 = (s32[16]{0:T(128)S(1)}, s32[16]{0:T(128)S(1)}, u32[]{:S(2)}, u32[]{:S(2)}) collective-permute-start(s32[16]{0:T(128)S(1)} %get-tuple-element.28), channel_id=1, source_target_pairs={{0,8},{8,16},{16,24},{24,32},{32,40},{40,48},{48,56},{56,64},{64,7... | collective-permute-start | bytes 200 | tf_op jit(solution)/shard_map/ppermute | solution.py:58
  49.7 0.5 collective-permute-done.4
  50.5 1.6 convert_element_type.46
  52.4 1.6 convert_element_type.52
  54.5 1.7 fusion.18
  56.3 1.6 constant_dynamic-update-slice_fusion.2
  58.0 0.4 fusion.15
  58.4 1.6 constant_dynamic-update-slice_fusion.1
  60.2 1.8 fusion.13
  62.0 1.6 constant_dynamic-update-slice_fusion
  63.6 3.3 %constant_dynamic-slice_fusion.2 = (bf16[1,128,48,128]{3,2,1,0:T(8,128)(2,1)S(1)}, bf16[1,128,48,128]{3,2,1,0:T(8,128)(2,1)S(1)}, bf16[1,128,48,128]{3,2,1,0:T(8...) fusion(bf16[6,128,48,128]{3,2,1,0:T(8,128)(2,1)S(1)} %constant_, ...), kind=kLoop, calls=%fused_computation.69 | loop fusion | bytes 18874392 | tf_op jit(solution)/shard_map/jit(dynamic_index_in_dim)/dynamic_slice | solution.py:93
  66.9 2.5 %multiply_convert_fusion = bf16[3,128,48,128]{3,2,1,0:T(8,128)(2,1)S(1)} fusion(bf16[1,128,48,128]{3,2,1,0:T(8,128)(2,1)S(1)} %get-tuple-element.8, bf16[1,128,48,128]{3,2,1,0:T(8,128)(2,1)} %get-tuple-element.9, bf16[1,128,48,128]{3,2,1,0:T(8,128)(2,1)} %get-tuple-element.10, f32[48]{0:T(128)S(1)} %broadcast_divide_fusion), kind=kLoop, calls=%fused_computation.7 | loop fusion | flops 11796480 | bytes 9437376 | tf_op jit(solution)/shard_map/convert_element_type | solution.py:95
  69.5 0.6 slice_bitcast_fusion.3
  70.1 0.6 pad_maximum_fusion.1
  70.7 2.9 %slice_bitcast_fusion.1 = (bf16[1,3,64,48,128]{4,3,0,2,1:T(8,128)(2,1)}, bf16[1,3,64,48,128]{4,3,0,2,1:T(8,128)(2,1)}) fusion(bf16[3,128,48,128]{3,2,1,0:T(8,128)(2,1)S(1)} %pad_maximum_fusion.1), kind=kLoop, calls=%fused_computation.23 | loop fusion | bytes 9437184 | tf_op jit(solution)/shard_map/stack | solution.py:99
  73.6 2.9 %maximum_bitcast_fusion = (bf16[1,2,3,64,48,128]{5,4,3,2,1,0:T(8,128)(2,1)S(1)}, bf16[1,2,3,64,48,128]{5,4,3,2,1,0:T(8,128)(2,1)}) fusion(bf16[1,3,64,48,128]{4,3,2,1,0:T(8,128)(2,1)S(1)} %get-tuple-element.15, bf16[1,3,64,48,128]{4,3,2,1,0:T(8,128)(2,1)S(1)} %get-tuple-element.13, bf16[1,3,64,48,128]{4,3,2,1,0:T(8,128)(2,1)S(1)} %get-tuple-element.14), kind=kLoop, calls=%fused_computation.8 | loop fusion | flops 4718592 | bytes 16515072 | tf_op jit(solution)/shard_map/stack | solution.py:98
  76.5 12.4 %convolution_bitcast_fusion = f32[3,64,2,16,8,128]{5,4,3,2,1,0:T(8,128)} fusion(bf16[1,3,64,48,128]{4,3,0,2,1:T(8,128)(2,1)} %get-tuple-element.12, bf16[1,3,64,48,128]{4,3,0,2,1:T(8,128)(2,1)} %get-tuple-element.11, bf16[1,2,3,64,48,128]{5,4,3,2,1,0:T(8,128)(2,1)} %get-tuple-element.19, bf16[1,2,3,64,48,128]{5,4,3,2,1,0:T(8,128)(2,1)S(1)} %get-tuple-element.18), kind=kOutput, calls=%fused_computation.4 | convolution fusion | flops 1215037440 | bytes 39321600 | tf_op jit(solution)/shard_map/qpskwc,pskwd->skqcd/dot_general | solution.py:100
  88.9 32.8 %fusion.2 = f32[16,3,8,64,128]{4,3,2,1,0:T(8,128)} fusion(f32[3]{0:T(128)S(1)} %compare_convert_fusion, f32[3,64,2,16,8,128]{5,4,3,2,1,0:T(8,128)} %convolution_bitcast_fusion, f32[2,64,64,1,1,1]{1,0,2,5,4,3:T(2,128)S(1)} %bitcast.75), kind=kOutput, calls=%fused_computation.3 | convolution fusion | flops 2419064832 | bytes 37781516 | tf_op jit(solution)/shard_map/skqgcd,qkl->gscld/dot_general | solution.py:106
  121.8 100.4 %reduce-scatter.4.cloned.1.call-done = f32[1,3,8,64,128]{4,3,2,1,0:T(8,128)} async-done(((f32[16,3,8,64,128]{4,3,2,1,0:T(8,128)}), f32[1,3,8,64,128]{4,3,2,1,0:T(8,128)}) %reduce-scatter.4.cloned.1.call-update) | async-done | bytes 786448
  (39 shorter events, 2.5 us)
Async XLA Ops:
  6.5 215.7 %reduce-scatter.4.cloned.1.call-start = ((), (), s32[]{:S(2)}) async-start(), calls=%async_computation.1 | async-start | bytes 13369344
  10.9 39.6 %collective-permute-start = (bf16[48,1,128,128]{2,0,3,1:T(8,128)(2,1)S(1)}, bf16[48,1,128,128]{2,0,3,1:T(8,128)(2,1)}, u32[]{:S(2)}, u32[]{:S(2)}) collective-permute-start(bf16[48,1,128,128]{2,0,3,1:T(8,128)(2,1)S(1)} %copy.41), channel_id=1, source_target_pairs={{0,1},{1,2},{2,3},{3,4},{4,5},{5,6},{6,7},{8,9},{9,10},{10,11},{11... | collective-permute-start | bytes 4718600 | tf_op jit(solution)/shard_map/ppermute | solution.py:73
  15.9 36.6 %collective-permute-start.2 = (bf16[48,1,128,128]{2,0,3,1:T(8,128)(2,1)S(1)}, bf16[48,1,128,128]{2,0,3,1:T(8,128)(2,1)}, u32[]{:S(2)}, u32[]{:S(2)}) collective-permute-start(bf16[48,1,128,128]{2,0,3,1:T(8,128)(2,1)S(1)} %copy.41), channel_id=1, source_target_pairs={{1,0},{2,1},{3,2},{4,3},{5,4},{6,5},{7,6},{9,8},{10,9},{11,10},{12... | collective-permute-start | bytes 4718600 | tf_op jit(solution)/shard_map/ppermute | solution.py:74
  22.9 7.2 %copy-start.1 = (s32[48]{0:T(128)S(1)}, s32[48]{0:T(128)}, u32[]{:S(2)}) copy-start(s32[48]{0:T(128)} %param.5) | copy-start | bytes 580
  24.5 31.7 %collective-permute-start.1 = (bf16[1,128,48,128]{3,2,1,0:T(8,128)(2,1)}, bf16[1,128,48,128]{3,2,1,0:T(8,128)(2,1)}, u32[]{:S(2)}, u32[]{:S(2)}) collective-permute-start(bf16[1,128,48,128]{3,2,1,0:T(8,128)(2,1)} %fusion.16), channel_id=1, source_target_pairs={{0,1},{1,2},{2,3},{3,4},{4,5},{5,6},{6,7},{8,9},{9,10},{10,11},{11... | collective-permute-start | bytes 4718600 | tf_op jit(solution)/shard_map/ppermute | solution.py:77
  28.2 33.9 %collective-permute-start.3 = (bf16[1,128,48,128]{3,2,1,0:T(8,128)(2,1)}, bf16[1,128,48,128]{3,2,1,0:T(8,128)(2,1)}, u32[]{:S(2)}, u32[]{:S(2)}) collective-permute-start(bf16[1,128,48,128]{3,2,1,0:T(8,128)(2,1)} %fusion.16), channel_id=1, source_target_pairs={{1,0},{2,1},{3,2},{4,3},{5,4},{6,5},{7,6},{9,8},{10,9},{11,10},{12... | collective-permute-start | bytes 4718600 | tf_op jit(solution)/shard_map/ppermute | solution.py:80
  30.2 15.3 %collective-permute-start.5 = (s32[16]{0:T(128)S(1)}, s32[16]{0:T(128)S(1)}, u32[]{:S(2)}, u32[]{:S(2)}) collective-permute-start(s32[16]{0:T(128)S(1)} %get-tuple-element.29), channel_id=1, source_target_pairs={{8,0},{16,8},{24,16},{32,24},{40,32},{48,40},{56,48},{64,56},{72,6... | collective-permute-start | bytes 200 | tf_op jit(solution)/shard_map/ppermute | solution.py:59
  31.7 0.7 copy-start
  45.5 4.7 %collective-permute-start.4 = (s32[16]{0:T(128)S(1)}, s32[16]{0:T(128)S(1)}, u32[]{:S(2)}, u32[]{:S(2)}) collective-permute-start(s32[16]{0:T(128)S(1)} %get-tuple-element.28), channel_id=1, source_target_pairs={{0,8},{8,16},{16,24},{24,32},{32,40},{40,48},{48,56},{56,64},{64,7... | collective-permute-start | bytes 200 | tf_op jit(solution)/shard_map/ppermute | solution.py:58
Sparse Core Ops, SparseCore 0:
  121.9 100.2 reduce-scatter.3

commit v9 on v6

--- a/solution.py
+++ b/solution.py
@@ -66,7 +66,9 @@
 def on_device(spectra, segment_ids, pair_blocks, pair_count):
     weight = window_weight(segment_ids)
     block_count = spectra.shape[1]
-    pieces = [whiten_transposed(spectra[:, i : i + 1]) for i in range(block_count)]
+    blocks = [spectra[:, i : i + 1] for i in range(block_count)]
+    blocks[1], weight = lax.optimization_barrier((blocks[1], weight))
+    pieces = [whiten_transposed(block) for block in blocks]
     count = lax.axis_size("tile")
     up = [(i, i + 1) for i in range(count - 1)]
     down = [(j, i) for i, j in up]

time: 223 us -> 236 us (1.058)
  waiting for transfers between devices: 101 us -> 112 us
    ppermute x2, waiting for transfers between devices: 0.01 us -> 10 us  [on_device(): after = [lax.ppermute(piece, 'tile', down) for piece in pieces]]
    ppermute x2, waiting for transfers between devices: 0.01 us -> 4.81 us  [on_device(): before = [lax.ppermute(piece, 'tile', up) for piece in pieces]]
    unnamed x11 -> x10, local copies, waits for them, and re-layouts: 9.61 us -> 6.16 us
    unnamed x2, waiting for transfers between devices: 100 us -> 97.5 us
  transfers between devices with their start and end apart: 7 -> 7, of which waited for: 2 -> 3; matrix products, arithmetic and copies ran while one was open for 7% -> 8% of each run, Pallas kernels for 0% -> 0%
where the time goes in v9:
time: 236 us; the launch traced here: 235 us
  waiting for transfers between devices  112 us (47%)
  matrix products  45.3 us (19%)
  between operations  25.9 us (11%)
  local copies, waits for them, and re-layouts  20.4 us (9%)
  starting transfers between devices  18.3 us (8%)
  other arithmetic  13.2 us (6%)
    unnamed x2, waiting for transfers between devices  97.5 us
    dot_general x1, matrix products, on_device(): jnp.einsum('skqgcd,qkl->gscld', cross, basis, precision=lax.Precision.HIGH)  32.9 us
    dot_general x1, matrix products, on_device(): jnp.einsum('qpskwc,pskwd->skqcd', left_both, right_both, preferred_elemen...  12.5 us
    ppermute x2, waiting for transfers between devices, on_device(): after = [lax.ppermute(piece, 'tile', down) for piece in pieces]  10 us
    ppermute x2, starting transfers between devices, on_device(): before = [lax.ppermute(piece, 'tile', up) for piece in pieces]  6.82 us
    unnamed x10, local copies, waits for them, and re-layouts  6.16 us
    ppermute x2, starting transfers between devices, on_device(): after = [lax.ppermute(piece, 'tile', down) for piece in pieces]  5.66 us
    ppermute x2, waiting for transfers between devices, on_device(): before = [lax.ppermute(piece, 'tile', up) for piece in pieces]  4.81 us
  transfers between devices with their start and end apart: 7, of which 3 were waited for; matrix products, arithmetic and copies ran while one was open for 8% of the time, Pallas kernels for 0%

profile of v9, /device:TPU:1, one launch (start us, length us, event | category | flops | bytes accessed | tf_op | source)
XLA Modules:
  0.0 235.5 jit_solution(1413550596902441706)
XLA Ops:
  6.5 0.7 broadcast_add_fusion.2
  7.3 1.3 collective-permute-start.2
  8.6 4.6 %collective-permute-start.1 = (s32[16]{0:T(128)S(1)}, s32[16]{0:T(128)S(1)}, u32[]{:S(2)}, u32[]{:S(2)}) collective-permute-start(s32[16]{0:T(128)S(1)} %get-tuple-element.32), channel_id=1, source_target_pairs={{0,8},{8,16},{16,24},{24,32},{32,40},{40,48},{48,56},{56,64},{64,7... | collective-permute-start | bytes 200 | tf_op jit(solution)/shard_map/ppermute | solution.py:58
  13.1 3.4 %fusion.20 = (bf16[48,1,128,128]{3,2,1,0:T(8,128)(2,1)}, bf16[48,1,128,128]{3,2,1,0:T(8,128)(2,1)S(1)}) fusion(bf16[48,2,128,128]{3,2,1,0:T(8,128)(2,1)} %param.4), kind=kLoop, calls=%fused_computation.68 | loop fusion | bytes 6291456 | tf_op jit(solution)/shard_map/slice | solution.py:69
  16.5 1.0 copy.41
  17.5 0.2 convert_element_type.34
  18.2 0.3 fusion.11
  18.5 4.9 %collective-permute-start = (bf16[1,128,48,128]{3,2,1,0:T(8,128)(2,1)S(1)}, bf16[1,128,48,128]{3,2,1,0:T(8,128)(2,1)}, u32[]{:S(2)}, u32[]{:S(2)}) collective-permute-start(bf16[1,128,48,128]{3,2,1,0:T(8,128)(2,1)S(1)} %fusion.11), channel_id=1, source_target_pairs={{0,1},{1,2},{2,3},{3,4},{4,5},{5,6},{6,7},{8,9},{9,10},{10,11},{11... | collective-permute-start | bytes 4718600 | tf_op jit(solution)/shard_map/ppermute | solution.py:75
  23.4 2.0 copy.42
  25.8 0.2 convert_element_type.37
  26.0 1.3 fusion.12
  27.4 1.5 reduce_sum.29
  29.0 1.5 fusion.10
  30.5 1.9 collective-permute-start.3
  32.4 3.6 %collective-permute-start.4 = (bf16[1,128,48,128]{3,2,1,0:T(8,128)(2,1)S(1)}, bf16[1,128,48,128]{3,2,1,0:T(8,128)(2,1)S(1)}, u32[]{:S(2)}, u32[]{:S(2)}) collective-permute-start(bf16[1,128,48,128]{3,2,1,0:T(8,128)(2,1)S(1)} %fusion.11), channel_id=1, source_target_pairs={{1,0},{2,1},{3,2},{4,3},{5,4},{6,5},{7,6},{9,8},{10,9},{11,10},{12... | collective-permute-start | bytes 4718600 | tf_op jit(solution)/shard_map/ppermute | solution.py:76
  36.0 2.1 collective-permute-start.5
  38.1 0.7 fusion.21
  51.4 1.5 constant_dynamic-update-slice_fusion.5
  52.9 4.8 %collective-permute-done.3 = bf16[1,128,48,128]{3,2,1,0:T(8,128)(2,1)} collective-permute-done((bf16[1,128,48,128]{3,2,1,0:T(8,128)(2,1)}, bf16[1,128,48,128]{3,2,1,0:T(8,128)(2,1)}, u32[]{:S(2)}, u32[]{:S(2)}) %collective-permute-start.3) | collective-permute-done | bytes 1572896 | tf_op jit(solution)/shard_map/ppermute | solution.py:75
  57.7 1.6 constant_dynamic-update-slice_fusion.4
  59.6 1.6 constant_dynamic-update-slice_fusion.2
  61.4 10.0 %collective-permute-done.5 = bf16[1,128,48,128]{3,2,1,0:T(8,128)(2,1)} collective-permute-done((bf16[1,128,48,128]{3,2,1,0:T(8,128)(2,1)}, bf16[1,128,48,128]{3,2,1,0:T(8,128)(2,1)}, u32[]{:S(2)}, u32[]{:S(2)}) %collective-permute-start.5) | collective-permute-done | bytes 1572896 | tf_op jit(solution)/shard_map/ppermute | solution.py:76
  71.4 1.6 constant_dynamic-update-slice_fusion
  73.0 3.3 %constant_dynamic-slice_fusion.2 = (bf16[1,128,48,128]{3,2,1,0:T(8,128)(2,1)S(1)}, bf16[1,128,48,128]{3,2,1,0:T(8,128)(2,1)S(1)}, bf16[1,128,48,128]{3,2,1,0:T(8...) fusion(bf16[6,128,48,128]{3,2,1,0:T(8,128)(2,1)S(1)} %constant_, ...), kind=kLoop, calls=%fused_computation.55 | loop fusion | bytes 18874392 | tf_op jit(solution)/shard_map/jit(dynamic_index_in_dim)/dynamic_slice | solution.py:88
  76.3 2.5 %multiply_convert_fusion = bf16[3,128,48,128]{3,2,1,0:T(8,128)(2,1)S(1)} fusion(bf16[1,128,48,128]{3,2,1,0:T(8,128)(2,1)S(1)} %get-tuple-element.12, bf16[1,128,48,128]{3,2,1,0:T(8,128)(2,1)} %get-tuple-element.13, bf16[1,128,48,128]{3,2,1,0:T(8,128)(2,1)} %get-tuple-element.14, f32[48]{0:T(128)S(1)} %broadcast_divide_fusion), kind=kLoop, calls=%fused_computation.7 | loop fusion | flops 11796480 | bytes 9437376 | tf_op jit(solution)/shard_map/convert_element_type | solution.py:90
  78.8 0.6 slice_bitcast_fusion.3
  79.4 0.6 pad_maximum_fusion.1
  80.0 2.9 %slice_bitcast_fusion.1 = (bf16[1,3,64,48,128]{4,3,0,2,1:T(8,128)(2,1)}, bf16[1,3,64,48,128]{4,3,0,2,1:T(8,128)(2,1)}) fusion(bf16[3,128,48,128]{3,2,1,0:T(8,128)(2,1)S(1)} %pad_maximum_fusion.1), kind=kLoop, calls=%fused_computation.19 | loop fusion | bytes 9437184 | tf_op jit(solution)/shard_map/stack | solution.py:94
  82.9 2.9 %maximum_bitcast_fusion = (bf16[1,2,3,64,48,128]{5,4,3,2,1,0:T(8,128)(2,1)S(1)}, bf16[1,2,3,64,48,128]{5,4,3,2,1,0:T(8,128)(2,1)}) fusion(bf16[1,3,64,48,128]{4,3,2,1,0:T(8,128)(2,1)S(1)} %get-tuple-element.19, bf16[1,3,64,48,128]{4,3,2,1,0:T(8,128)(2,1)S(1)} %get-tuple-element.17, bf16[1,3,64,48,128]{4,3,2,1,0:T(8,128)(2,1)S(1)} %get-tuple-element.18), kind=kLoop, calls=%fused_computation.8 | loop fusion | flops 4718592 | bytes 16515072 | tf_op jit(solution)/shard_map/stack | solution.py:93
  85.8 12.5 %convolution_bitcast_fusion = f32[3,64,2,16,8,128]{5,4,3,2,1,0:T(8,128)} fusion(bf16[1,3,64,48,128]{4,3,0,2,1:T(8,128)(2,1)} %get-tuple-element.16, bf16[1,3,64,48,128]{4,3,0,2,1:T(8,128)(2,1)} %get-tuple-element.15, bf16[1,2,3,64,48,128]{5,4,3,2,1,0:T(8,128)(2,1)} %get-tuple-element.23, bf16[1,2,3,64,48,128]{5,4,3,2,1,0:T(8,128)(2,1)S(1)} %get-tuple-element.22), kind=kOutput, calls=%fused_computation.4 | convolution fusion | flops 1215037440 | bytes 39321600 | tf_op jit(solution)/shard_map/qpskwc,pskwd->skqcd/dot_general | solution.py:95
  98.3 32.9 %fusion.2 = f32[16,3,8,64,128]{4,3,2,1,0:T(8,128)} fusion(f32[3]{0:T(128)S(1)} %compare_convert_fusion, f32[3,64,2,16,8,128]{5,4,3,2,1,0:T(8,128)} %convolution_bitcast_fusion, f32[2,64,64,1,1,1]{1,0,2,5,4,3:T(2,128)S(1)} %bitcast.57), kind=kOutput, calls=%fused_computation.3 | convolution fusion | flops 2419064832 | bytes 37781516 | tf_op jit(solution)/shard_map/skqgcd,qkl->gscld/dot_general | solution.py:101
  131.1 97.5 %reduce-scatter.4.cloned.1.call-done = f32[1,3,8,64,128]{4,3,2,1,0:T(8,128)} async-done(((f32[16,3,8,64,128]{4,3,2,1,0:T(8,128)}), f32[1,3,8,64,128]{4,3,2,1,0:T(8,128)}) %reduce-scatter.4.cloned.1.call-update) | async-done | bytes 786448
  (30 shorter events, 1.7 us)
Async XLA Ops:
  6.5 222.1 %reduce-scatter.4.cloned.1.call-start = ((), (), s32[]{:S(2)}) async-start(), calls=%async_computation.1 | async-start | bytes 13369344
  7.3 18.2 %collective-permute-start.2 = (s32[16]{0:T(128)S(1)}, s32[16]{0:T(128)S(1)}, u32[]{:S(2)}, u32[]{:S(2)}) collective-permute-start(s32[16]{0:T(128)S(1)} %get-tuple-element.33), channel_id=1, source_target_pairs={{8,0},{16,8},{24,16},{32,24},{40,32},{48,40},{56,48},{64,56},{72,6... | collective-permute-start | bytes 200 | tf_op jit(solution)/shard_map/ppermute | solution.py:59
  8.6 16.9 %collective-permute-start.1 = (s32[16]{0:T(128)S(1)}, s32[16]{0:T(128)S(1)}, u32[]{:S(2)}, u32[]{:S(2)}) collective-permute-start(s32[16]{0:T(128)S(1)} %get-tuple-element.32), channel_id=1, source_target_pairs={{0,8},{8,16},{16,24},{24,32},{32,40},{40,48},{48,56},{56,64},{64,7... | collective-permute-start | bytes 200 | tf_op jit(solution)/shard_map/ppermute | solution.py:58
  18.2 7.3 %copy-start.1 = (s32[48]{0:T(128)S(1)}, s32[48]{0:T(128)}, u32[]{:S(2)}) copy-start(s32[48]{0:T(128)} %param.5) | copy-start | bytes 580
  18.5 32.9 %collective-permute-start = (bf16[1,128,48,128]{3,2,1,0:T(8,128)(2,1)S(1)}, bf16[1,128,48,128]{3,2,1,0:T(8,128)(2,1)}, u32[]{:S(2)}, u32[]{:S(2)}) collective-permute-start(bf16[1,128,48,128]{3,2,1,0:T(8,128)(2,1)S(1)} %fusion.11), channel_id=1, source_target_pairs={{0,1},{1,2},{2,3},{3,4},{4,5},{5,6},{6,7},{8,9},{9,10},{10,11},{11... | collective-permute-start | bytes 4718600 | tf_op jit(solution)/shard_map/ppermute | solution.py:75
  28.9 9.2 %copy-start = (s32[3,2]{0,1:T(2,128)S(1)}, s32[3,2]{0,1:T(2,128)}, u32[]{:S(2)}) copy-start(s32[3,2]{0,1:T(2,128)} %param.6) | copy-start | bytes 76
  30.5 27.2 %collective-permute-start.3 = (bf16[1,128,48,128]{3,2,1,0:T(8,128)(2,1)}, bf16[1,128,48,128]{3,2,1,0:T(8,128)(2,1)}, u32[]{:S(2)}, u32[]{:S(2)}) collective-permute-start(bf16[1,128,48,128]{3,2,1,0:T(8,128)(2,1)} %fusion.10), channel_id=1, source_target_pairs={{0,1},{1,2},{2,3},{3,4},{4,5},{5,6},{6,7},{8,9},{9,10},{10,11},{11... | collective-permute-start | bytes 4718600 | tf_op jit(solution)/shard_map/ppermute | solution.py:75
  32.4 28.8 %collective-permute-start.4 = (bf16[1,128,48,128]{3,2,1,0:T(8,128)(2,1)S(1)}, bf16[1,128,48,128]{3,2,1,0:T(8,128)(2,1)S(1)}, u32[]{:S(2)}, u32[]{:S(2)}) collective-permute-start(bf16[1,128,48,128]{3,2,1,0:T(8,128)(2,1)S(1)} %fusion.11), channel_id=1, source_target_pairs={{1,0},{2,1},{3,2},{4,3},{5,4},{6,5},{7,6},{9,8},{10,9},{11,10},{12... | collective-permute-start | bytes 4718600 | tf_op jit(solution)/shard_map/ppermute | solution.py:76
  36.0 35.4 %collective-permute-start.5 = (bf16[1,128,48,128]{3,2,1,0:T(8,128)(2,1)}, bf16[1,128,48,128]{3,2,1,0:T(8,128)(2,1)}, u32[]{:S(2)}, u32[]{:S(2)}) collective-permute-start(bf16[1,128,48,128]{3,2,1,0:T(8,128)(2,1)} %fusion.10), channel_id=1, source_target_pairs={{1,0},{2,1},{3,2},{4,3},{5,4},{6,5},{7,6},{9,8},{10,9},{11,10},{12... | collective-permute-start | bytes 4718600 | tf_op jit(solution)/shard_map/ppermute | solution.py:76
Sparse Core Ops, SparseCore 0:
  131.3 97.3 reduce-scatter.3
